TPU v7x, 128 devices: a whole 4x4x4 slice. The times are simulated.
128 devices in a mesh: gx: 8 (over z, core), gy: 16 (over y, x).
Axes of the slice: x: 4, y: 4, z: 4, core: 2. Of those that a mesh axis runs over, the one named last changes fastest.
Arguments:
- records: bfloat16 [98304, 2048], P(('gx', 'gy')), may hold values from -4000 to 4000
- record_owner: int32 [98304], P(('gx', 'gy')), may hold values from 0 to 127, as said below
- record_field: int32 [98304], P(('gx', 'gy')), may hold values from 0 to 767, as said below
- filter_taps: float32 [2, 9], replicated, may hold values from 0.02 to 0.3
Outputs:
- modes: float32 [256, 3, 262144], P(None, None, ('gx', 'gy'))
- r_factor: float32 [256, 256], replicated
- first_factor: float32 [256, 256], replicated
Inputs may be any that keep to these rules, and one draw needn't show every extreme that they name: `record_owner`: A device sends at most 12 records to any one owner; every device sends exactly 12 records to the owner whose index is its own plus 128 / 2, counted round; every owner is named by exactly 768 records over all devices. `record_field`: over all devices each pair of owner and field number occurs in exactly one record; field number 3 * s + c holds velocity component c of snapshot s.
All inputs are finite; a program needn't handle non-finite values.
Results may differ from a plain program's by a relative error of at most 0.0003.
Values may be sent and summed in bfloat16 or wider, within the bound.
No kernel may reach another device: no remote copies, remote signals or barrier semaphores. Data moves between devices by JAX's collectives and lax.ppermute only.
A program may use at most 128 MiB of HBM per device.

v0:
```python
import functools
import math

import jax
import jax.numpy as jnp
from jax import lax
from jax.experimental import pallas as pl
from jax.experimental.pallas import tpu as pltpu
from jax.sharding import PartitionSpec as P

SNAP = 256
PX = 16
PZ = 128


def circulant(tap_row, period):
    places = jnp.arange(period, dtype=jnp.int32)
    offsets = jnp.arange(9, dtype=jnp.int32) - 4
    target = (places[None, :, None] + offsets[:, None, None]) % period
    onehot = (target == places[None, None, :]).astype(jnp.float32)
    return jnp.einsum("k,kxa->xa", tap_row, onehot, precision=lax.Precision.HIGHEST)


def split_three(matrix):
    high = lax.reduce_precision(matrix, exponent_bits=8, mantissa_bits=7)
    rest = matrix - high
    mid = lax.reduce_precision(rest, exponent_bits=8, mantissa_bits=7)
    low = rest - mid
    return jnp.concatenate([high, mid, low], axis=1).astype(jnp.bfloat16)


def filter_kernel(taps_ref, span_ref, planes_ref, out_ref, gram_ref, spread_ref):
    taps = taps_ref.shape[1]
    reach = (taps - 1) // 2
    span = span_ref[...]

    @pl.when(pl.program_id(0) == 0)
    def _():
        gram_ref[...] = jnp.zeros(gram_ref.shape, jnp.float32)

    for x in range(PX):
        parts = jnp.dot(planes_ref[x], span, preferred_element_type=jnp.float32)
        spread_ref[x] = parts[:, :PZ] + parts[:, PZ : 2 * PZ] + parts[:, 2 * PZ :]
    for x in range(PX):
        acc = taps_ref[0, 0] * spread_ref[(x - reach) % PX]
        for k in range(1, taps):
            acc = acc + taps_ref[0, k] * spread_ref[(x + k - reach) % PX]
        out_ref[:, x * PZ : (x + 1) * PZ] = acc
    block = out_ref[...]
    gram_ref[...] += lax.dot_general(
        block,
        block,
        (((1,), (1,)), ((), ())),
        precision=lax.Precision.HIGHEST,
        preferred_element_type=jnp.float32,
    )


def filter_planes(planes, filter_taps):
    count = planes.shape[1]
    span = split_three(circulant(filter_taps[1], PZ).T)
    return pl.pallas_call(
        filter_kernel,
        grid=(count // SNAP,),
        in_specs=[
            pl.BlockSpec(memory_space=pltpu.SMEM),
            pl.BlockSpec((PZ, 3 * PZ), lambda i: (0, 0)),
            pl.BlockSpec((PX, SNAP, PZ), lambda i: (0, i, 0)),
        ],
        out_specs=[
            pl.BlockSpec((SNAP, PX * PZ), lambda i: (i, 0)),
            pl.BlockSpec((SNAP, SNAP), lambda i: (0, 0)),
        ],
        out_shape=[
            jax.ShapeDtypeStruct((count, PX * PZ), jnp.float32),
            jax.ShapeDtypeStruct((SNAP, SNAP), jnp.float32),
        ],
        scratch_shapes=[pltpu.VMEM((PX, SNAP, PZ), jnp.float32)],
    )(filter_taps, span, planes)


def basis_kernel(inv_ref, matrix_ref, basis_ref, gram_ref):
    @pl.when(pl.program_id(0) == 0)
    def _():
        gram_ref[...] = jnp.zeros(gram_ref.shape, jnp.float32)

    basis = jnp.dot(
        inv_ref[...],
        matrix_ref[...],
        precision=lax.Precision.HIGHEST,
        preferred_element_type=jnp.float32,
    )
    basis_ref[...] = basis
    gram_ref[...] += lax.dot_general(
        basis,
        basis,
        (((1,), (1,)), ((), ())),
        precision=lax.Precision.HIGHEST,
        preferred_element_type=jnp.float32,
    )


def basis_and_gram(inverse, matrix):
    count, width = matrix.shape
    size = inverse.shape[0]
    return pl.pallas_call(
        basis_kernel,
        grid=(count // size,),
        in_specs=[
            pl.BlockSpec((size, size), lambda i: (0, 0)),
            pl.BlockSpec((size, width), lambda i: (i, 0)),
        ],
        out_specs=[
            pl.BlockSpec((size, width), lambda i: (i, 0)),
            pl.BlockSpec((size, size), lambda i: (0, 0)),
        ],
        out_shape=[
            jax.ShapeDtypeStruct((count, width), jnp.float32),
            jax.ShapeDtypeStruct((size, size), jnp.float32),
        ],
    )(inverse, matrix)


def modes_kernel(inv_ref, basis_ref, modes_ref, *, scale):
    modes_ref[...] = (
        jnp.dot(
            inv_ref[...],
            basis_ref[...],
            precision=lax.Precision.HIGHEST,
            preferred_element_type=jnp.float32,
        )
        * scale
    )


def modes_of(inverse, basis, scale):
    count, width = basis.shape
    size = inverse.shape[0]
    return pl.pallas_call(
        functools.partial(modes_kernel, scale=scale),
        grid=(count // size,),
        in_specs=[
            pl.BlockSpec((size, size), lambda i: (0, 0)),
            pl.BlockSpec((size, width), lambda i: (i, 0)),
        ],
        out_specs=pl.BlockSpec((size, width), lambda i: (i, 0)),
        out_shape=jax.ShapeDtypeStruct((count, width), jnp.float32),
    )(inverse, basis)


def swap_kernel(planes_ref, records_ref):
    records_ref[...] = pltpu.einshape("akb->kab", planes_ref[...])


def planes_to_records(planes, rows=256):
    width, count, lanes = planes.shape
    return pl.pallas_call(
        swap_kernel,
        grid=(count // rows,),
        in_specs=[pl.BlockSpec((width, rows, lanes), lambda i: (0, i, 0))],
        out_specs=pl.BlockSpec((rows, width, lanes), lambda i: (i, 0, 0)),
        out_shape=jax.ShapeDtypeStruct((count, width, lanes), planes.dtype),
    )(planes)


def gram_of(matrix):
    return lax.dot_general(
        matrix,
        matrix,
        (((1,), (1,)), ((), ())),
        precision=lax.Precision.HIGHEST,
        preferred_element_type=jnp.float32,
    )


def high_dot(a, b, dims):
    return lax.dot_general(
        a, b, (dims, ((), ())), precision=lax.Precision.HIGHEST, preferred_element_type=jnp.float32
    )


def factor_and_inverse(gram):
    half = gram.shape[0] // 2
    gram = (gram + gram.T) / 2
    eye = jnp.eye(half, dtype=jnp.float32)
    lower_a = lax.linalg.cholesky(gram[:half, :half], symmetrize_input=False)
    inv_a = jnp.tril(lax.linalg.triangular_solve(lower_a, eye, left_side=True, lower=True))
    lower_b = high_dot(gram[half:, :half], inv_a, ((1,), (1,)))
    rest = gram[half:, half:] - high_dot(lower_b, lower_b, ((1,), (1,)))
    lower_c = lax.linalg.cholesky(rest, symmetrize_input=False)
    inv_c = jnp.tril(lax.linalg.triangular_solve(lower_c, eye, left_side=True, lower=True))
    inv_b = -high_dot(inv_c, high_dot(lower_b, inv_a, ((1,), (0,))), ((1,), (0,)))
    zero = jnp.zeros((half, half), jnp.float32)
    lower = jnp.block([[lower_a, zero], [lower_b, lower_c]])
    inverse = jnp.block([[inv_a, zero], [inv_b, inv_c]])
    return lower, inverse


def sum_over_devices(part, axes, devices_all):
    rows = part.reshape(devices_all, -1)
    rows = lax.all_to_all(rows, axes, 0, 0, tiled=True)
    total = jnp.sum(rows, axis=0, keepdims=True)
    total = jnp.broadcast_to(total, rows.shape)
    total = lax.all_to_all(total, axes, 0, 0, tiled=True)
    return total.reshape(part.shape)


def local(records, record_owner, record_field, filter_taps):
    devices_all = lax.axis_size(("gx", "gy"))
    rec_count = records.shape[0]
    cells = records.shape[1]
    capacity = 2 * (rec_count // devices_all)
    onehot = (record_owner[:, None] == jnp.arange(devices_all, dtype=jnp.int32)[None, :]).astype(
        jnp.int32
    )
    position = jnp.sum((jnp.cumsum(onehot, axis=0) - 1) * onehot, axis=1)
    slot = record_owner * capacity + position
    places = jnp.arange(devices_all * capacity, dtype=jnp.int32)
    pick = slot[None, :] == places[:, None]
    buffer = jnp.einsum(
        "kr,rab->akb",
        pick.astype(jnp.bfloat16),
        records.reshape(rec_count, PX, PZ),
        preferred_element_type=jnp.float32,
    ).astype(jnp.bfloat16)
    buffer = planes_to_records(buffer)
    labels = jnp.sum(jnp.where(pick, record_field[None, :] + 1, 0), axis=1) - 1
    arrived, arrived_labels = (
        lax.all_to_all(
            buffer.reshape(devices_all, capacity, PX, PZ),
            ("gx", "gy"),
            split_axis=0,
            concat_axis=0,
            tiled=True,
        ),
        lax.all_to_all(
            labels.reshape(devices_all, capacity),
            ("gx", "gy"),
            split_axis=0,
            concat_axis=0,
            tiled=True,
        ),
    )
    flat_data = arrived.reshape(devices_all * capacity, PX, PZ)
    flat_labels = arrived_labels.reshape(devices_all * capacity)
    target = (flat_labels % 3) * SNAP + flat_labels // 3
    target = jnp.where(flat_labels >= 0, target, -1)
    order = target[None, :] == jnp.arange(rec_count, dtype=jnp.int32)[:, None]
    planes = jnp.einsum(
        "tk,kab->atb", order.astype(jnp.bfloat16), flat_data, preferred_element_type=jnp.float32
    ).astype(jnp.bfloat16)
    fields, gram_one = filter_planes(planes, filter_taps)
    lower_one, inv_one = factor_and_inverse(sum_over_devices(gram_one, ("gx", "gy"), devices_all))
    basis_one, gram_two = basis_and_gram(inv_one, fields)
    lower_two, inv_two = factor_and_inverse(sum_over_devices(gram_two, ("gx", "gy"), devices_all))
    scale = math.sqrt(3.0 * cells * devices_all)
    modes = modes_of(inv_two, basis_one, scale).reshape(3, SNAP, cells)
    r_factor = (
        jnp.dot(
            lower_two.T,
            lower_one.T,
            precision=lax.Precision.HIGHEST,
            preferred_element_type=jnp.float32,
        )
        / scale
    )
    first_factor = lower_one.T / scale
    return (modes.transpose(1, 0, 2), r_factor, first_factor)


def solution(mesh):
    placed = (P(("gx", "gy"), None), P(("gx", "gy")), P(("gx", "gy")), P())
    return jax.shard_map(
        local,
        mesh=mesh,
        in_specs=placed,
        out_specs=(P(None, None, ("gx", "gy")), P(), P()),
        check_vma=False,
    )
```

profile of v0, /device:TPU:1, one launch (start us, length us, event | category | flops | bytes accessed | tf_op | source)
XLA Modules:
  0.0 348.5 jit_solution(13760579049258705443)
XLA Ops:
  0.6 0.9 copy.33
  1.8 0.8 copy-done.1
  2.6 1.1 add_add_fusion
  3.8 1.0 fusion.18
  6.1 0.7 sub.42
  6.8 11.5 %all-to-all-start.1 = ((s32[128,1,12]{2,1,0:T(1,128)}), s32[128,1,12]{2,1,0:T(1,128)S(1)}, u32[]{:S(2)}, u32[]{:S(2)}) async-start(s32[128,1,12]{2,1,0:T(1,128)} %bitcast.13), calls=%async_computation.1 | async-start | bytes 131072 | tf_op jit(solution)/shard_map/all_to_all | solution.py:236
  18.3 6.9 %convert_bitcast_fusion.planes_ref = bf16[16,1536,128]{2,1,0:T(8,128)(2,1)} fusion(s32[768]{0:T(1024)S(1)} %get-tuple-element.37, bf16[768,2048]{1,0:T(8,128)(2,1)S(1)} %copy-done), kind=kOutput, calls=%fused_computation.2 | convolution fusion | flops 4836163584 | bytes 9440256 | tf_op jit(solution)/shard_map/kr,rab->akb/dot_general | solution.py:220
  25.2 7.4 %shard_map.67 = bf16[1536,16,128]{2,1,0:T(8,128)(2,1)} custom-call(bf16[16,1536,128]{2,1,0:T(8,128)(2,1)} %convert_bitcast_fusion.planes_ref), custom_call_target="tpu_custom_call" | custom-call | tf_op jit(solution)/shard_map/pallas_call | solution.py:157
  32.7 10.9 %all-to-all-start = ((bf16[128,12,16,128]{3,2,1,0:T(8,128)(2,1)}), bf16[128,12,16,128]{3,2,1,0:T(8,128)(2,1)}, u32[]{:S(2)}, u32[]{:S(2)}) async-start(bf16[128,12,16,128]{3,2,1,0:T(8,128)(2,1)} %bitcast.93), calls=%async_computation | async-start | bytes 12582912 | tf_op jit(solution)/shard_map/all_to_all | solution.py:229
  46.7 71.2 %all-to-all-done = bf16[128,12,16,128]{3,2,1,0:T(8,128)(2,1)} async-done(((bf16[128,12,16,128]{3,2,1,0:T(8,128)(2,1)}), bf16[128,12,16,128]{3,2,1,0:T(8,128)(2,1)}, u32[]{:S(2)}, u32[]{:S(2)}) %all-to-all-start) | async-done | bytes 6291488 | tf_op jit(solution)/shard_map/all_to_all | solution.py:229
  117.9 9.5 %convert_bitcast_fusion.1.planes_ref = bf16[16,768,128]{2,1,0:T(8,128)(2,1)} fusion(s32[1536]{0:T(1024)S(1)} %fusion.48, bf16[1536,16,128]{2,1,0:T(8,128)(2,1)} %bitcast.12), kind=kOutput, calls=%fused_computation.10 | convolution fusion | flops 4834590720 | bytes 9443328 | tf_op jit(solution)/shard_map/tk,kab->atb/dot_general | solution.py:249
  127.4 14.6 %shard_map.68 = (f32[768,2048]{1,0:T(8,128)}, f32[256,256]{1,0:T(8,128)}) custom-call(f32[2,9]{1,0:T(2,128)} %taps_ref.1, bf16[128,384]{1,0:T(8,128)(2,1)} %pad_maximum_fusion.span_ref, bf16[16,768,128]{2,1,0:T(8,128)(2,1)} %convert_bitcast_fusion.1.planes_ref), custom_call_target="tpu_custom_call" | custom-call | tf_op jit(solution)/shard_map/pallas_call | solution.py:62
  142.0 1.2 all_to_all.35
  143.2 17.0 %all_to_all.43 = f32[128,1,512]{2,1,0:T(1,128)} all-to-all(f32[128,1,512]{2,1,0:T(1,128)S(1)} %all_to_all.35), channel_id=1, replica_groups=mesh['gx'=8,'gy'=16] {'gx','gy'}, dimensions={0} | all-to-all | bytes 524288 | tf_op jit(solution)/shard_map/all_to_all | solution.py:201
  160.2 1.2 reduce_sum.38
  161.6 15.3 %all_to_all.44 = f32[128,1,512]{2,1,0:T(1,128)S(1)} all-to-all(f32[128,1,512]{2,1,0:T(1,128)S(1)} %broadcast_in_dim.24), channel_id=1, replica_groups=mesh['gx'=8,'gy'=16] {'gx','gy'}, dimensions={0} | all-to-all | bytes 524288 | tf_op jit(solution)/shard_map/all_to_all | solution.py:204
  176.8 1.3 reduce.42
  178.2 1.0 reshape.182
  179.2 0.8 copy.40
  180.0 1.0 fusion.24
  181.7 11.7 %custom-call.12 = f32[128,128]{1,0:T(8,128)S(1)} custom-call(f32[128,128]{1,0:T(8,128)S(1)} %slice.41), custom_call_target="Cholesky" | custom-call | tf_op jit(solution)/shard_map/cholesky/custom-call.1 | solution.py:186
  194.8 9.8 %custom-call.13 = f32[1,128,128]{1,2,0:T(8,128)S(1)} custom-call(f32[1,128,128]{2,1,0:T(8,128)S(1)} %get-tuple-element.32), custom_call_target="InvertDiagBlocksLowerTriangular" | custom-call | tf_op jit(solution)/shard_map/triangular_solve/custom-call.0 | solution.py:187
  204.9 1.1 fusion.35
  206.0 1.1 convolution_subtract_fusion.1
  207.4 11.7 %custom-call.14 = f32[128,128]{1,0:T(8,128)S(1)} custom-call(f32[128,128]{1,0:T(8,128)S(1)} %convolution_subtract_fusion.1), custom_call_target="Cholesky" | custom-call | tf_op jit(solution)/shard_map/cholesky/custom-call.1 | solution.py:190
  219.8 1.3 select_bitcast_fusion.2
  221.1 10.0 %custom-call.15 = f32[1,128,128]{1,2,0:T(8,128)S(1)} custom-call(f32[1,128,128]{2,1,0:T(8,128)S(1)} %get-tuple-element.30), custom_call_target="InvertDiagBlocksLowerTriangular" | custom-call | tf_op jit(solution)/shard_map/triangular_solve/custom-call.0 | solution.py:191
  232.3 14.3 %shard_map.69 = (f32[768,2048]{1,0:T(8,128)}, f32[256,256]{1,0:T(8,128)}) custom-call(f32[256,256]{1,0:T(8,128)} %select_maximum_fusion.4.inv_ref, f32[768,2048]{1,0:T(8,128)} %get-tuple-element.10.matrix_ref), custom_call_target="tpu_custom_call" | custom-call | tf_op jit(solution)/shard_map/pallas_call | solution.py:106
  246.6 1.9 all_to_all.36
  248.5 15.7 %all_to_all.45 = f32[128,1,512]{2,1,0:T(1,128)S(1)} all-to-all(f32[128,1,512]{2,1,0:T(1,128)} %all_to_all.36), channel_id=1, replica_groups=mesh['gx'=8,'gy'=16] {'gx','gy'}, dimensions={0} | all-to-all | bytes 524288 | tf_op jit(solution)/shard_map/all_to_all | solution.py:201
  264.4 0.8 broadcast_in_dim.26
  265.3 4.4 %all-to-all-start.5 = ((f32[128,1,512]{2,1,0:T(1,128)}), f32[128,1,512]{2,1,0:T(1,128)S(1)}, u32[]{:S(2)}, u32[]{:S(2)}) async-start(f32[128,1,512]{2,1,0:T(1,128)} %broadcast_in_dim.26), calls=%async_computation.5 | async-start | bytes 524288 | tf_op jit(solution)/shard_map/all_to_all | solution.py:204
  270.4 1.6 multiply_bitcast_fusion
  272.0 1.8 copy.49
  273.8 7.0 %all-to-all-done.5 = f32[128,1,512]{2,1,0:T(1,128)S(1)} async-done(((f32[128,1,512]{2,1,0:T(1,128)}), f32[128,1,512]{2,1,0:T(1,128)S(1)}, u32[]{:S(2)}, u32[]{:S(2)}) %all-to-all-start.5) | async-done | bytes 262176 | tf_op jit(solution)/shard_map/all_to_all | solution.py:204
  280.8 1.3 reduce.43
  282.1 1.0 reshape.183
  283.1 0.8 copy.44
  284.0 1.0 fusion.23
  285.7 11.7 %custom-call.16 = f32[128,128]{1,0:T(8,128)S(1)} custom-call(f32[128,128]{1,0:T(8,128)S(1)} %slice.44), custom_call_target="Cholesky" | custom-call | tf_op jit(solution)/shard_map/cholesky/custom-call.1 | solution.py:186
  298.7 9.8 %custom-call.17 = f32[1,128,128]{1,2,0:T(8,128)S(1)} custom-call(f32[1,128,128]{2,1,0:T(8,128)S(1)} %get-tuple-element.28), custom_call_target="InvertDiagBlocksLowerTriangular" | custom-call | tf_op jit(solution)/shard_map/triangular_solve/custom-call.0 | solution.py:187
  308.8 1.1 fusion.33
  309.9 1.1 convolution_subtract_fusion
  312.1 11.7 %custom-call.18 = f32[128,128]{1,0:T(8,128)S(1)} custom-call(f32[128,128]{1,0:T(8,128)S(1)} %convolution_subtract_fusion), custom_call_target="Cholesky" | custom-call | tf_op jit(solution)/shard_map/cholesky/custom-call.1 | solution.py:190
  324.5 1.3 select_bitcast_fusion
  325.7 11.1 %custom-call.19 = f32[1,128,128]{1,2,0:T(8,128)S(1)} custom-call(f32[1,128,128]{2,1,0:T(8,128)} %get-tuple-element.26), custom_call_target="InvertDiagBlocksLowerTriangular" | custom-call | tf_op jit(solution)/shard_map/triangular_solve/custom-call.0 | solution.py:191
  338.1 9.0 %shard_map.70 = f32[768,2048]{1,0:T(8,128)} custom-call(f32[256,256]{1,0:T(8,128)} %select_maximum_fusion.3.inv_ref, f32[768,2048]{1,0:T(8,128)} %get-tuple-element.12.basis_ref), custom_call_target="tpu_custom_call" | custom-call | tf_op jit(solution)/shard_map/pallas_call | solution.py:139
  347.1 1.2 convolution_multiply_fusion
  (63 shorter events, 15.5 us)
Async XLA Ops:
  0.6 17.7 %copy-start = (bf16[768,2048]{1,0:T(8,128)(2,1)S(1)}, bf16[768,2048]{1,0:T(8,128)(2,1)}, u32[]{:S(2)}) copy-start(bf16[768,2048]{1,0:T(8,128)(2,1)} %param.7) | copy-start | bytes 9437188
  1.8 0.8 copy-start.1
  6.8 25.8 %all-to-all-start.1 = ((s32[128,1,12]{2,1,0:T(1,128)}), s32[128,1,12]{2,1,0:T(1,128)S(1)}, u32[]{:S(2)}, u32[]{:S(2)}) async-start(s32[128,1,12]{2,1,0:T(1,128)} %bitcast.13), calls=%async_computation.1 | async-start | bytes 131072 | tf_op jit(solution)/shard_map/all_to_all | solution.py:236
  32.7 11.2 %copy-start.7 = (f32[2,9]{1,0:T(2,128)S(1)}, f32[2,9]{1,0:T(2,128)}, u32[]{:S(2)}) copy-start(f32[2,9]{1,0:T(2,128)} %taps_ref.1) | copy-start | bytes 220
  32.7 85.2 %all-to-all-start = ((bf16[128,12,16,128]{3,2,1,0:T(8,128)(2,1)}), bf16[128,12,16,128]{3,2,1,0:T(8,128)(2,1)}, u32[]{:S(2)}, u32[]{:S(2)}) async-start(bf16[128,12,16,128]{3,2,1,0:T(8,128)(2,1)} %bitcast.93), calls=%async_computation | async-start | bytes 12582912 | tf_op jit(solution)/shard_map/all_to_all | solution.py:229
  181.0 0.7 copy-start.2
  265.3 15.5 %all-to-all-start.5 = ((f32[128,1,512]{2,1,0:T(1,128)}), f32[128,1,512]{2,1,0:T(1,128)S(1)}, u32[]{:S(2)}, u32[]{:S(2)}) async-start(f32[128,1,512]{2,1,0:T(1,128)} %broadcast_in_dim.26), calls=%async_computation.5 | async-start | bytes 524288 | tf_op jit(solution)/shard_map/all_to_all | solution.py:204
  284.9 0.7 copy-start.3
  338.1 9.1 %copy-start.4 = (f32[128,128]{1,0:T(8,128)S(1)}, f32[128,128]{1,0:T(8,128)}, u32[]{:S(2)}) copy-start(f32[128,128]{1,0:T(8,128)} %get-tuple-element.31) | copy-start | bytes 196612
  338.1 9.1 %copy-start.5 = (f32[128,128]{1,0:T(8,128)S(1)}, f32[128,128]{1,0:T(8,128)}, u32[]{:S(2)}) copy-start(f32[128,128]{1,0:T(8,128)} %copy.48) | copy-start | bytes 196612
  338.1 9.1 %copy-start.6 = (f32[128,128]{1,0:T(8,128)S(1)}, f32[128,128]{1,0:T(8,128)}, u32[]{:S(2)}) copy-start(f32[128,128]{1,0:T(8,128)} %copy.47) | copy-start | bytes 196612
where the time goes:
time: 354 us; the launch traced here: 348 us
  other arithmetic  109 us (31%)
  waiting for transfers between devices  78.1 us (22%)
  blocking collectives  48 us (14%)
  Pallas kernels  45.4 us (13%)
  starting transfers between devices  26.8 us (8%)
  matrix products  24.7 us (7%)
  local copies, waits for them, and re-layouts  15.5 us (4%)
    all_to_all x1, waiting for transfers between devices, local(): lax.all_to_all(buffer.reshape(devices_all, capacity, PX, PZ), ('gx', 'gy'...  71.2 us
    all_to_all x2, blocking collectives, sum_over_devices(): rows = lax.all_to_all(rows, axes, 0, 0, tiled=True)  32.8 us
    another operation x6, other arithmetic, factor_and_inverse(): lower_c = lax.linalg.cholesky(rest, symmetrize_input=False)  24.8 us
    another operation x6, other arithmetic, factor_and_inverse(): lower_a = lax.linalg.cholesky(gram[:half, :half], symmetrize_input=False)  24.8 us
    another operation x4, other arithmetic, factor_and_inverse(): lax.linalg.triangular_solve(lower_c, eye, left_side=True, lower=True)  23.6 us
    another operation x4, other arithmetic, factor_and_inverse(): lax.linalg.triangular_solve(lower_a, eye, left_side=True, lower=True)  20.9 us
    all_to_all x1, blocking collectives, sum_over_devices(): total = lax.all_to_all(total, axes, 0, 0, tiled=True)  15.3 us
    pallas_call x1, Pallas kernels, filter_planes(): pl.pallas_call(filter_kernel, grid=(count // SNAP,), in_specs=[pl.BlockSp...  14.6 us
  transfers between devices with their start and end apart: 3, of which 2 were waited for; matrix products, arithmetic and copies ran while one was open for 4% of the time, Pallas kernels for 2%

commit v1 on v0

--- a/solution.py
+++ b/solution.py
@@ -163,6 +163,33 @@
     )(planes)
 
 
+def tri_inverse_kernel(lower_ref, inverse_ref):
+    lower = lower_ref[...]
+    size = lower.shape[0]
+    row = lax.broadcasted_iota(jnp.int32, lower.shape, 0)
+    col = lax.broadcasted_iota(jnp.int32, lower.shape, 1)
+    inverse = jnp.where(row == col, 1.0 / lower, 0.0)
+    level = 0
+    while (1 << level) < size:
+        same_pair = lax.shift_right_logical(row, level + 1) == lax.shift_right_logical(col, level + 1)
+        other_half = lax.shift_right_logical(row, level) != lax.shift_right_logical(col, level)
+        coupling = jnp.where(same_pair & other_half, lower, 0.0)
+        step = jnp.dot(
+            inverse, coupling, precision=lax.Precision.HIGHEST, preferred_element_type=jnp.float32
+        )
+        inverse = inverse - jnp.dot(
+            step, inverse, precision=lax.Precision.HIGHEST, preferred_element_type=jnp.float32
+        )
+        level += 1
+    inverse_ref[...] = inverse
+
+
+def tri_inverse(lower):
+    return pl.pallas_call(
+        tri_inverse_kernel, out_shape=jax.ShapeDtypeStruct(lower.shape, jnp.float32)
+    )(lower)
+
+
 def gram_of(matrix):
     return lax.dot_general(
         matrix,
@@ -182,13 +209,12 @@
 def factor_and_inverse(gram):
     half = gram.shape[0] // 2
     gram = (gram + gram.T) / 2
-    eye = jnp.eye(half, dtype=jnp.float32)
     lower_a = lax.linalg.cholesky(gram[:half, :half], symmetrize_input=False)
-    inv_a = jnp.tril(lax.linalg.triangular_solve(lower_a, eye, left_side=True, lower=True))
+    inv_a = tri_inverse(lower_a)
     lower_b = high_dot(gram[half:, :half], inv_a, ((1,), (1,)))
     rest = gram[half:, half:] - high_dot(lower_b, lower_b, ((1,), (1,)))
     lower_c = lax.linalg.cholesky(rest, symmetrize_input=False)
-    inv_c = jnp.tril(lax.linalg.triangular_solve(lower_c, eye, left_side=True, lower=True))
+    inv_c = tri_inverse(lower_c)
     inv_b = -high_dot(inv_c, high_dot(lower_b, inv_a, ((1,), (0,))), ((1,), (0,)))
     zero = jnp.zeros((half, half), jnp.float32)
     lower = jnp.block([[lower_a, zero], [lower_b, lower_c]])

time: 354 us -> 337 us (0.952)
  other arithmetic: 109 us -> 71 us
  Pallas kernels: 45.4 us -> 63 us
    another operation x11 -> x3, other arithmetic: 44.8 us -> 0.25 us  [the longest x4 23.6 us: factor_and_inverse(): lax.linalg.triangular_solve(lower_c, eye, left_side=True, lower=True)]
    pallas_call x0 -> x4, Pallas kernels: none -> 17.7 us  [tri_inverse(): pl.pallas_call(tri_inverse_kernel, out_shape=jax.ShapeDtypeStruct(lower.s...]
    select_n x0 -> x4, other arithmetic: none -> 5.03 us  [the longest x2 2.54 us: factor_and_inverse(): lower_c = lax.linalg.cholesky(rest, symmetrize_input=False)]
    dot_general x8, matrix products: 5.44 us -> 9.05 us  [high_dot(): lax.dot_general(a, b, (dims, ((), ())), precision=lax.Precision.HIGHEST,...]
where the time goes in v1:
time: 337 us; the launch traced here: 331 us
  waiting for transfers between devices  78.4 us (23%)
  other arithmetic  71 us (21%)
  Pallas kernels  63 us (19%)
  blocking collectives  48 us (14%)
  matrix products  28.1 us (8%)
  starting transfers between devices  26.2 us (8%)
  local copies, waits for them, and re-layouts  14.9 us (4%)
    all_to_all x1, waiting for transfers between devices, local(): lax.all_to_all(buffer.reshape(devices_all, capacity, PX, PZ), ('gx', 'gy'...  71.2 us
    all_to_all x2, blocking collectives, sum_over_devices(): rows = lax.all_to_all(rows, axes, 0, 0, tiled=True)  32.8 us
    another operation x6, other arithmetic, factor_and_inverse(): lower_a = lax.linalg.cholesky(gram[:half, :half], symmetrize_input=False)  24.8 us
    another operation x6, other arithmetic, factor_and_inverse(): lower_c = lax.linalg.cholesky(rest, symmetrize_input=False)  24.8 us
    pallas_call x4, Pallas kernels, tri_inverse(): pl.pallas_call(tri_inverse_kernel, out_shape=jax.ShapeDtypeStruct(lower.s...  17.7 us
    all_to_all x1, blocking collectives, sum_over_devices(): total = lax.all_to_all(total, axes, 0, 0, tiled=True)  15.3 us
    pallas_call x1, Pallas kernels, filter_planes(): pl.pallas_call(filter_kernel, grid=(count // SNAP,), in_specs=[pl.BlockSp...  14.6 us
    pallas_call x1, Pallas kernels, basis_and_gram(): pl.pallas_call(basis_kernel, grid=(count // size,), in_specs=[pl.BlockSpe...  14.3 us
  transfers between devices with their start and end apart: 3, of which 2 were waited for; matrix products, arithmetic and copies ran while one was open for 4% of the time, Pallas kernels for 2%

profile of v1, /device:TPU:1, one launch (start us, length us, event | category | flops | bytes accessed | tf_op | source)
XLA Modules:
  0.0 330.8 jit_solution(12196549989062175311)
XLA Ops:
  2.6 1.1 add_add_fusion
  6.8 11.5 %all-to-all-start.1 = ((s32[128,1,12]{2,1,0:T(1,128)}), s32[128,1,12]{2,1,0:T(1,128)S(1)}, u32[]{:S(2)}, u32[]{:S(2)}) async-start(s32[128,1,12]{2,1,0:T(1,128)} %bitcast.13), calls=%async_computation.1 | async-start | bytes 131072 | tf_op jit(solution)/shard_map/all_to_all | solution.py:262
  18.3 6.9 %convert_bitcast_fusion.planes_ref = bf16[16,1536,128]{2,1,0:T(8,128)(2,1)} fusion(s32[768]{0:T(1024)S(1)} %get-tuple-element.28, bf16[768,2048]{1,0:T(8,128)(2,1)S(1)} %copy-done), kind=kOutput, calls=%fused_computation.2 | convolution fusion | flops 4836163584 | bytes 9440256 | tf_op jit(solution)/shard_map/kr,rab->akb/dot_general | solution.py:246
  25.2 7.4 %shard_map.67 = bf16[1536,16,128]{2,1,0:T(8,128)(2,1)} custom-call(bf16[16,1536,128]{2,1,0:T(8,128)(2,1)} %convert_bitcast_fusion.planes_ref), custom_call_target="tpu_custom_call" | custom-call | tf_op jit(solution)/shard_map/pallas_call | solution.py:157
  32.6 10.5 %all-to-all-start = ((bf16[128,12,16,128]{3,2,1,0:T(8,128)(2,1)}), bf16[128,12,16,128]{3,2,1,0:T(8,128)(2,1)}, u32[]{:S(2)}, u32[]{:S(2)}) async-start(bf16[128,12,16,128]{3,2,1,0:T(8,128)(2,1)} %bitcast.73), calls=%async_computation | async-start | bytes 12582912 | tf_op jit(solution)/shard_map/all_to_all | solution.py:255
  46.4 71.2 %all-to-all-done = bf16[128,12,16,128]{3,2,1,0:T(8,128)(2,1)} async-done(((bf16[128,12,16,128]{3,2,1,0:T(8,128)(2,1)}), bf16[128,12,16,128]{3,2,1,0:T(8,128)(2,1)}, u32[]{:S(2)}, u32[]{:S(2)}) %all-to-all-start) | async-done | bytes 6291488 | tf_op jit(solution)/shard_map/all_to_all | solution.py:255
  117.5 9.5 %convert_bitcast_fusion.1.planes_ref = bf16[16,768,128]{2,1,0:T(8,128)(2,1)} fusion(s32[1536]{0:T(1024)S(1)} %fusion.40, bf16[1536,16,128]{2,1,0:T(8,128)(2,1)} %bitcast.12), kind=kOutput, calls=%fused_computation.10 | convolution fusion | flops 4834590720 | bytes 9443328 | tf_op jit(solution)/shard_map/tk,kab->atb/dot_general | solution.py:275
  127.0 14.6 %shard_map.68 = (f32[768,2048]{1,0:T(8,128)}, f32[256,256]{1,0:T(8,128)}) custom-call(f32[2,9]{1,0:T(2,128)} %taps_ref.1, bf16[128,384]{1,0:T(8,128)(2,1)} %pad_maximum_fusion.span_ref, bf16[16,768,128]{2,1,0:T(8,128)(2,1)} %convert_bitcast_fusion.1.planes_ref), custom_call_target="tpu_custom_call" | custom-call | tf_op jit(solution)/shard_map/pallas_call | solution.py:62
  141.6 1.2 all_to_all.35
  142.9 17.0 %all_to_all.43 = f32[128,1,512]{2,1,0:T(1,128)} all-to-all(f32[128,1,512]{2,1,0:T(1,128)S(1)} %all_to_all.35), channel_id=1, replica_groups=mesh['gx'=8,'gy'=16] {'gx','gy'}, dimensions={0} | all-to-all | bytes 524288 | tf_op jit(solution)/shard_map/all_to_all | solution.py:227
  159.9 1.2 reduce_sum.38
  161.2 15.3 %all_to_all.44 = f32[128,1,512]{2,1,0:T(1,128)S(1)} all-to-all(f32[128,1,512]{2,1,0:T(1,128)S(1)} %broadcast_in_dim.20), channel_id=1, replica_groups=mesh['gx'=8,'gy'=16] {'gx','gy'}, dimensions={0} | all-to-all | bytes 524288 | tf_op jit(solution)/shard_map/all_to_all | solution.py:230
  176.5 1.3 reduce.42
  177.8 1.0 reshape.176
  179.6 1.0 fusion.24
  181.3 11.7 %custom-call.6 = f32[128,128]{1,0:T(8,128)S(1)} custom-call(f32[128,128]{1,0:T(8,128)S(1)} %slice.39), custom_call_target="Cholesky" | custom-call | tf_op jit(solution)/shard_map/cholesky/custom-call.1 | solution.py:212
  193.7 1.3 select_select_fusion.3.lower_ref
  195.0 4.4 %shard_map.69 = f32[128,128]{1,0:T(8,128)} custom-call(f32[128,128]{1,0:T(8,128)} %select_select_fusion.3.lower_ref), custom_call_target="tpu_custom_call" | custom-call | tf_op jit(solution)/shard_map/pallas_call | solution.py:188
  199.4 1.1 fusion.31
  200.5 1.1 convolution_subtract_fusion.1
  201.7 1.1 fusion.47
  202.8 11.7 %custom-call.7 = f32[128,128]{1,0:T(8,128)S(1)} custom-call(f32[128,128]{1,0:T(8,128)S(1)} %convolution_subtract_fusion.1), custom_call_target="Cholesky" | custom-call | tf_op jit(solution)/shard_map/cholesky/custom-call.1 | solution.py:216
  215.2 1.3 select_select_fusion.2.lower_ref
  216.5 4.4 %shard_map.70 = f32[128,128]{1,0:T(8,128)} custom-call(f32[128,128]{1,0:T(8,128)} %select_select_fusion.2.lower_ref), custom_call_target="tpu_custom_call" | custom-call | tf_op jit(solution)/shard_map/pallas_call | solution.py:188
  220.8 1.2 convolution_negate_fusion.1
  222.1 1.6 select_maximum_fusion.4.inv_ref
  223.7 14.3 %shard_map.71 = (f32[768,2048]{1,0:T(8,128)}, f32[256,256]{1,0:T(8,128)}) custom-call(f32[256,256]{1,0:T(8,128)} %select_maximum_fusion.4.inv_ref, f32[768,2048]{1,0:T(8,128)} %get-tuple-element.9.matrix_ref), custom_call_target="tpu_custom_call" | custom-call | tf_op jit(solution)/shard_map/pallas_call | solution.py:106
  238.0 1.9 all_to_all.36
  239.9 15.7 %all_to_all.45 = f32[128,1,512]{2,1,0:T(1,128)S(1)} all-to-all(f32[128,1,512]{2,1,0:T(1,128)} %all_to_all.36), channel_id=1, replica_groups=mesh['gx'=8,'gy'=16] {'gx','gy'}, dimensions={0} | all-to-all | bytes 524288 | tf_op jit(solution)/shard_map/all_to_all | solution.py:227
  256.7 4.2 %all-to-all-start.5 = ((f32[128,1,512]{2,1,0:T(1,128)}), f32[128,1,512]{2,1,0:T(1,128)S(1)}, u32[]{:S(2)}, u32[]{:S(2)}) async-start(f32[128,1,512]{2,1,0:T(1,128)} %broadcast_in_dim.21), calls=%async_computation.5 | async-start | bytes 524288 | tf_op jit(solution)/shard_map/all_to_all | solution.py:230
  261.6 1.6 multiply_bitcast_fusion
  263.2 1.8 copy.43
  265.0 7.2 %all-to-all-done.5 = f32[128,1,512]{2,1,0:T(1,128)S(1)} async-done(((f32[128,1,512]{2,1,0:T(1,128)}), f32[128,1,512]{2,1,0:T(1,128)S(1)}, u32[]{:S(2)}, u32[]{:S(2)}) %all-to-all-start.5) | async-done | bytes 262176 | tf_op jit(solution)/shard_map/all_to_all | solution.py:230
  272.2 1.3 reduce.43
  273.5 1.0 reshape.177
  277.1 11.7 %custom-call.8 = f32[128,128]{1,0:T(8,128)S(1)} custom-call(f32[128,128]{1,0:T(8,128)S(1)} %slice.42), custom_call_target="Cholesky" | custom-call | tf_op jit(solution)/shard_map/cholesky/custom-call.1 | solution.py:212
  289.5 1.2 select_select_fusion.1.lower_ref
  290.7 4.4 %shard_map.72 = f32[128,128]{1,0:T(8,128)} custom-call(f32[128,128]{1,0:T(8,128)} %select_select_fusion.1.lower_ref), custom_call_target="tpu_custom_call" | custom-call | tf_op jit(solution)/shard_map/pallas_call | solution.py:188
  295.0 1.1 fusion.29
  296.2 1.1 convolution_subtract_fusion
  297.4 1.1 fusion.48
  298.5 11.7 %custom-call.9 = f32[128,128]{1,0:T(8,128)S(1)} custom-call(f32[128,128]{1,0:T(8,128)S(1)} %convolution_subtract_fusion), custom_call_target="Cholesky" | custom-call | tf_op jit(solution)/shard_map/cholesky/custom-call.1 | solution.py:216
  310.9 1.3 select_select_fusion.lower_ref
  312.2 4.6 %shard_map.73 = f32[128,128]{1,0:T(8,128)} custom-call(f32[128,128]{1,0:T(8,128)} %select_select_fusion.lower_ref), custom_call_target="tpu_custom_call" | custom-call | tf_op jit(solution)/shard_map/pallas_call | solution.py:188
  316.8 1.0 convolution_negate_fusion
  317.8 1.6 select_maximum_fusion.3.inv_ref
  319.4 2.1 convolution_multiply_fusion
  321.6 9.0 %shard_map.74 = f32[768,2048]{1,0:T(8,128)} custom-call(f32[256,256]{1,0:T(8,128)} %select_maximum_fusion.3.inv_ref, f32[768,2048]{1,0:T(8,128)} %get-tuple-element.11.basis_ref), custom_call_target="tpu_custom_call" | custom-call | tf_op jit(solution)/shard_map/pallas_call | solution.py:139
  (55 shorter events, 16.9 us)
Async XLA Ops:
  0.6 17.7 %copy-start = (bf16[768,2048]{1,0:T(8,128)(2,1)S(1)}, bf16[768,2048]{1,0:T(8,128)(2,1)}, u32[]{:S(2)}) copy-start(bf16[768,2048]{1,0:T(8,128)(2,1)} %param.5) | copy-start | bytes 9437188
  1.8 0.8 copy-start.1
  6.8 25.8 %all-to-all-start.1 = ((s32[128,1,12]{2,1,0:T(1,128)}), s32[128,1,12]{2,1,0:T(1,128)S(1)}, u32[]{:S(2)}, u32[]{:S(2)}) async-start(s32[128,1,12]{2,1,0:T(1,128)} %bitcast.13), calls=%async_computation.1 | async-start | bytes 131072 | tf_op jit(solution)/shard_map/all_to_all | solution.py:262
  32.6 10.9 %copy-start.5 = (f32[2,9]{1,0:T(2,128)S(1)}, f32[2,9]{1,0:T(2,128)}, u32[]{:S(2)}) copy-start(f32[2,9]{1,0:T(2,128)} %taps_ref.1) | copy-start | bytes 220
  32.6 84.9 %all-to-all-start = ((bf16[128,12,16,128]{3,2,1,0:T(8,128)(2,1)}), bf16[128,12,16,128]{3,2,1,0:T(8,128)(2,1)}, u32[]{:S(2)}, u32[]{:S(2)}) async-start(bf16[128,12,16,128]{3,2,1,0:T(8,128)(2,1)} %bitcast.73), calls=%async_computation | async-start | bytes 12582912 | tf_op jit(solution)/shard_map/all_to_all | solution.py:255
  180.6 0.7 copy-start.2
  220.8 40.8 %copy-start.4 = (f32[128,128]{1,0:T(8,128)S(1)}, f32[128,128]{1,0:T(8,128)}, u32[]{:S(2)}) copy-start(f32[128,128]{1,0:T(8,128)} %select_select_fusion.3.lower_ref) | copy-start | bytes 196612
  256.7 15.5 %all-to-all-start.5 = ((f32[128,1,512]{2,1,0:T(1,128)}), f32[128,1,512]{2,1,0:T(1,128)S(1)}, u32[]{:S(2)}, u32[]{:S(2)}) async-start(f32[128,1,512]{2,1,0:T(1,128)} %broadcast_in_dim.21), calls=%async_computation.5 | async-start | bytes 524288 | tf_op jit(solution)/shard_map/all_to_all | solution.py:230
  276.4 0.7 copy-start.3

commit v2 on v1

--- a/solution.py
+++ b/solution.py
@@ -163,8 +163,7 @@
     )(planes)
 
 
-def tri_inverse_kernel(lower_ref, inverse_ref):
-    lower = lower_ref[...]
+def doubling_inverse(lower):
     size = lower.shape[0]
     row = lax.broadcasted_iota(jnp.int32, lower.shape, 0)
     col = lax.broadcasted_iota(jnp.int32, lower.shape, 1)
@@ -181,13 +180,42 @@
             step, inverse, precision=lax.Precision.HIGHEST, preferred_element_type=jnp.float32
         )
         level += 1
-    inverse_ref[...] = inverse
-
-
-def tri_inverse(lower):
-    return pl.pallas_call(
-        tri_inverse_kernel, out_shape=jax.ShapeDtypeStruct(lower.shape, jnp.float32)
-    )(lower)
+    return inverse
+
+
+def nt_dot(a, b):
+    return lax.dot_general(
+        a, b, (((1,), (1,)), ((), ())), precision=lax.Precision.HIGHEST,
+        preferred_element_type=jnp.float32,
+    )
+
+
+def nn_dot(a, b):
+    return jnp.dot(a, b, precision=lax.Precision.HIGHEST, preferred_element_type=jnp.float32)
+
+
+def first_half_kernel(lower_a_ref, gram_ref, inv_a_ref, lower_b_ref, rest_ref):
+    half = lower_a_ref.shape[0]
+    inv_a = doubling_inverse(lower_a_ref[...])
+    inv_a_ref[...] = inv_a
+    lower_b = nt_dot(gram_ref[half:, :half], inv_a)
+    lower_b_ref[...] = lower_b
+    rest_ref[...] = gram_ref[half:, half:] - nt_dot(lower_b, lower_b)
+
+
+def second_half_kernel(lower_a_ref, lower_b_ref, lower_c_ref, inv_a_ref, lower_ref, inverse_ref):
+    half = lower_a_ref.shape[0]
+    inv_c = doubling_inverse(lower_c_ref[...])
+    inv_a = inv_a_ref[...]
+    zero = jnp.zeros((half, half), jnp.float32)
+    lower_ref[:half, :half] = lower_a_ref[...]
+    lower_ref[:half, half:] = zero
+    lower_ref[half:, :half] = lower_b_ref[...]
+    lower_ref[half:, half:] = lower_c_ref[...]
+    inverse_ref[:half, :half] = inv_a
+    inverse_ref[:half, half:] = zero
+    inverse_ref[half:, :half] = -nn_dot(inv_c, nn_dot(lower_b_ref[...], inv_a))
+    inverse_ref[half:, half:] = inv_c
 
 
 def gram_of(matrix):
@@ -207,18 +235,19 @@
 
 
 def factor_and_inverse(gram):
-    half = gram.shape[0] // 2
+    size = gram.shape[0]
+    half = size // 2
     gram = (gram + gram.T) / 2
     lower_a = lax.linalg.cholesky(gram[:half, :half], symmetrize_input=False)
-    inv_a = tri_inverse(lower_a)
-    lower_b = high_dot(gram[half:, :half], inv_a, ((1,), (1,)))
-    rest = gram[half:, half:] - high_dot(lower_b, lower_b, ((1,), (1,)))
+    square = jax.ShapeDtypeStruct((half, half), jnp.float32)
+    inv_a, lower_b, rest = pl.pallas_call(
+        first_half_kernel, out_shape=[square, square, square]
+    )(lower_a, gram)
     lower_c = lax.linalg.cholesky(rest, symmetrize_input=False)
-    inv_c = tri_inverse(lower_c)
-    inv_b = -high_dot(inv_c, high_dot(lower_b, inv_a, ((1,), (0,))), ((1,), (0,)))
-    zero = jnp.zeros((half, half), jnp.float32)
-    lower = jnp.block([[lower_a, zero], [lower_b, lower_c]])
-    inverse = jnp.block([[inv_a, zero], [inv_b, inv_c]])
+    full = jax.ShapeDtypeStruct((size, size), jnp.float32)
+    lower, inverse = pl.pallas_call(
+        second_half_kernel, out_shape=[full, full]
+    )(lower_a, lower_b, lower_c, inv_a)
     return lower, inverse
 
 

time: 337 us -> 332 us (0.985)
  matrix products: 28.1 us -> 19.3 us
    dot_general x8 -> x0, matrix products: 9.05 us -> none  [high_dot(): lax.dot_general(a, b, (dims, ((), ())), precision=lax.Precision.HIGHEST,...]
where the time goes in v2:
time: 332 us; the launch traced here: 326 us
  waiting for transfers between devices  79.5 us (24%)
  other arithmetic  70.7 us (21%)
  Pallas kernels  65.2 us (20%)
  blocking collectives  49.2 us (15%)
  starting transfers between devices  27.4 us (8%)
  matrix products  19.3 us (6%)
  local copies, waits for them, and re-layouts  14 us (4%)
    all_to_all x1, waiting for transfers between devices, local(): lax.all_to_all(buffer.reshape(devices_all, capacity, PX, PZ), ('gx', 'gy'...  71.2 us
    all_to_all x2, blocking collectives, sum_over_devices(): rows = lax.all_to_all(rows, axes, 0, 0, tiled=True)  33.4 us
    another operation x6, other arithmetic, factor_and_inverse(): lower_c = lax.linalg.cholesky(rest, symmetrize_input=False)  26.4 us
    another operation x6, other arithmetic, factor_and_inverse(): lower_a = lax.linalg.cholesky(gram[:half, :half], symmetrize_input=False)  24.9 us
    all_to_all x1, blocking collectives, sum_over_devices(): total = lax.all_to_all(total, axes, 0, 0, tiled=True)  15.7 us
    pallas_call x1, Pallas kernels, filter_planes(): pl.pallas_call(filter_kernel, grid=(count // SNAP,), in_specs=[pl.BlockSp...  14.6 us
    pallas_call x1, Pallas kernels, basis_and_gram(): pl.pallas_call(basis_kernel, grid=(count // size,), in_specs=[pl.BlockSpe...  14.3 us
    all_to_all x1, starting transfers between devices, local(): lax.all_to_all(labels.reshape(devices_all, capacity), ('gx', 'gy'), split...  11.5 us
  transfers between devices with their start and end apart: 3, of which 2 were waited for; matrix products, arithmetic and copies ran while one was open for 4% of the time, Pallas kernels for 2%

profile of v2, /device:TPU:1, one launch (start us, length us, event | category | flops | bytes accessed | tf_op | source)
XLA Modules:
  0.0 326.4 jit_solution(4743072513032135913)
XLA Ops:
  0.6 0.9 copy.21
  1.8 0.8 copy-done.1
  2.6 1.1 add_add_fusion
  3.8 1.0 fusion.18
  6.1 0.7 sub.36
  6.8 11.5 %all-to-all-start.1 = ((s32[128,1,12]{2,1,0:T(1,128)}), s32[128,1,12]{2,1,0:T(1,128)S(1)}, u32[]{:S(2)}, u32[]{:S(2)}) async-start(s32[128,1,12]{2,1,0:T(1,128)} %bitcast.13), calls=%async_computation.1 | async-start | bytes 131072 | tf_op jit(solution)/shard_map/all_to_all | solution.py:291
  18.3 6.9 %convert_bitcast_fusion.planes_ref = bf16[16,1536,128]{2,1,0:T(8,128)(2,1)} fusion(s32[768]{0:T(1024)S(1)} %get-tuple-element.48, bf16[768,2048]{1,0:T(8,128)(2,1)S(1)} %copy-done), kind=kOutput, calls=%fused_computation.2 | convolution fusion | flops 4836163584 | bytes 9440256 | tf_op jit(solution)/shard_map/kr,rab->akb/dot_general | solution.py:275
  25.2 7.4 %shard_map.67 = bf16[1536,16,128]{2,1,0:T(8,128)(2,1)} custom-call(bf16[16,1536,128]{2,1,0:T(8,128)(2,1)} %convert_bitcast_fusion.planes_ref), custom_call_target="tpu_custom_call" | custom-call | tf_op jit(solution)/shard_map/pallas_call | solution.py:157
  32.6 10.6 %all-to-all-start = ((bf16[128,12,16,128]{3,2,1,0:T(8,128)(2,1)}), bf16[128,12,16,128]{3,2,1,0:T(8,128)(2,1)}, u32[]{:S(2)}, u32[]{:S(2)}) async-start(bf16[128,12,16,128]{3,2,1,0:T(8,128)(2,1)} %bitcast.61), calls=%async_computation | async-start | bytes 12582912 | tf_op jit(solution)/shard_map/all_to_all | solution.py:284
  46.4 71.2 %all-to-all-done = bf16[128,12,16,128]{3,2,1,0:T(8,128)(2,1)} async-done(((bf16[128,12,16,128]{3,2,1,0:T(8,128)(2,1)}), bf16[128,12,16,128]{3,2,1,0:T(8,128)(2,1)}, u32[]{:S(2)}, u32[]{:S(2)}) %all-to-all-start) | async-done | bytes 6291488 | tf_op jit(solution)/shard_map/all_to_all | solution.py:284
  117.6 9.5 %convert_bitcast_fusion.1.planes_ref = bf16[16,768,128]{2,1,0:T(8,128)(2,1)} fusion(s32[1536]{0:T(1024)S(1)} %fusion.30, bf16[1536,16,128]{2,1,0:T(8,128)(2,1)} %bitcast.12), kind=kOutput, calls=%fused_computation.10 | convolution fusion | flops 4834590720 | bytes 9443328 | tf_op jit(solution)/shard_map/tk,kab->atb/dot_general | solution.py:304
  127.1 14.6 %shard_map.68 = (f32[768,2048]{1,0:T(8,128)}, f32[256,256]{1,0:T(8,128)}) custom-call(f32[2,9]{1,0:T(2,128)} %taps_ref.1, bf16[128,384]{1,0:T(8,128)(2,1)} %pad_maximum_fusion.span_ref, bf16[16,768,128]{2,1,0:T(8,128)(2,1)} %convert_bitcast_fusion.1.planes_ref), custom_call_target="tpu_custom_call" | custom-call | tf_op jit(solution)/shard_map/pallas_call | solution.py:62
  141.7 1.2 all_to_all.35
  142.9 17.0 %all_to_all.43 = f32[128,1,512]{2,1,0:T(1,128)} all-to-all(f32[128,1,512]{2,1,0:T(1,128)S(1)} %all_to_all.35), channel_id=1, replica_groups=mesh['gx'=8,'gy'=16] {'gx','gy'}, dimensions={0} | all-to-all | bytes 524288 | tf_op jit(solution)/shard_map/all_to_all | solution.py:256
  159.9 1.2 reduce_sum.38
  161.2 15.7 %all_to_all.44 = f32[128,1,512]{2,1,0:T(1,128)S(1)} all-to-all(f32[128,1,512]{2,1,0:T(1,128)S(1)} %broadcast_in_dim.20), channel_id=1, replica_groups=mesh['gx'=8,'gy'=16] {'gx','gy'}, dimensions={0} | all-to-all | bytes 524288 | tf_op jit(solution)/shard_map/all_to_all | solution.py:259
  177.0 1.3 reduce.42
  178.3 1.0 reshape.176
  179.3 0.8 copy.28
  180.1 1.0 fusion.20.gram_ref
  181.8 11.7 %custom-call.6 = f32[128,128]{1,0:T(8,128)S(1)} custom-call(f32[128,128]{1,0:T(8,128)S(1)} %slice.23), custom_call_target="Cholesky" | custom-call | tf_op jit(solution)/shard_map/cholesky/custom-call.1 | solution.py:241
  193.6 0.7 compare_reduce_fusion.5
  194.3 1.3 select_select_fusion.3.lower_a_ref
  195.6 5.2 %shard_map.69 = (f32[128,128]{1,0:T(8,128)}, f32[128,128]{1,0:T(8,128)}, f32[128,128]{1,0:T(8,128)}) custom-call(f32[128,128]{1,0:T(8,128)} %select_select_fusion.3.lower_a_ref, f32[256,256]{1,0:T(8,128)} %copy-done.2), custom_call_target="tpu_custom_call" | custom-call | tf_op jit(solution)/shard_map/pallas_call | solution.py:243
  200.8 12.5 %custom-call.7 = f32[128,128]{1,0:T(8,128)S(1)} custom-call(f32[128,128]{1,0:T(8,128)} %get-tuple-element.20), custom_call_target="Cholesky" | custom-call | tf_op jit(solution)/shard_map/cholesky/custom-call.1 | solution.py:246
  214.0 1.3 select_select_fusion.2.lower_c_ref
  215.3 4.8 %shard_map.70 = (f32[256,256]{1,0:T(8,128)}, f32[256,256]{1,0:T(8,128)}) custom-call(f32[128,128]{1,0:T(8,128)} %select_select_fusion.3.lower_a_ref, f32[128,128]{1,0:T(8,128)} %get-tuple-element.19.lower_b_ref, f32[128,128]{1,0:T(8,128)} %select_select_fusion.2.lower_c_ref, f32[128,128]{1,0:T(8,128)} %get-tuple-element.21.inv_a_ref), custom_call_target="tpu_custom_call" | custom-call | tf_op jit(solution)/shard_map/pallas_call | solution.py:248
  220.1 14.3 %shard_map.71 = (f32[768,2048]{1,0:T(8,128)}, f32[256,256]{1,0:T(8,128)}) custom-call(f32[256,256]{1,0:T(8,128)} %get-tuple-element.22.inv_ref, f32[768,2048]{1,0:T(8,128)} %get-tuple-element.23.matrix_ref), custom_call_target="tpu_custom_call" | custom-call | tf_op jit(solution)/shard_map/pallas_call | solution.py:106
  234.4 1.9 all_to_all.36
  236.3 16.4 %all_to_all.45 = f32[128,1,512]{2,1,0:T(1,128)} all-to-all(f32[128,1,512]{2,1,0:T(1,128)} %all_to_all.36), channel_id=1, replica_groups=mesh['gx'=8,'gy'=16] {'gx','gy'}, dimensions={0} | all-to-all | bytes 524288 | tf_op jit(solution)/shard_map/all_to_all | solution.py:256
  252.8 1.2 reduce_sum.39
  253.9 0.8 broadcast_in_dim.21
  254.8 5.3 %all-to-all-start.5 = ((f32[128,1,512]{2,1,0:T(1,128)}), f32[128,1,512]{2,1,0:T(1,128)}, u32[]{:S(2)}, u32[]{:S(2)}) async-start(f32[128,1,512]{2,1,0:T(1,128)} %broadcast_in_dim.21), calls=%async_computation.5 | async-start | bytes 524288 | tf_op jit(solution)/shard_map/all_to_all | solution.py:259
  260.1 0.7 multiply_bitcast_fusion
  260.8 1.8 copy.31
  262.6 8.4 %all-to-all-done.5 = f32[128,1,512]{2,1,0:T(1,128)} async-done(((f32[128,1,512]{2,1,0:T(1,128)}), f32[128,1,512]{2,1,0:T(1,128)}, u32[]{:S(2)}, u32[]{:S(2)}) %all-to-all-start.5) | async-done | bytes 262176 | tf_op jit(solution)/shard_map/all_to_all | solution.py:259
  270.9 2.3 reduce.43
  273.2 1.0 reshape.177
  274.2 0.8 copy.30
  275.1 1.0 fusion.19.gram_ref
  276.8 11.7 %custom-call.8 = f32[128,128]{1,0:T(8,128)S(1)} custom-call(f32[128,128]{1,0:T(8,128)S(1)} %slice.24), custom_call_target="Cholesky" | custom-call | tf_op jit(solution)/shard_map/cholesky/custom-call.1 | solution.py:241
  289.1 1.3 select_select_fusion.1.lower_a_ref
  290.4 5.2 %shard_map.72 = (f32[128,128]{1,0:T(8,128)}, f32[128,128]{1,0:T(8,128)}, f32[128,128]{1,0:T(8,128)}) custom-call(f32[128,128]{1,0:T(8,128)} %select_select_fusion.1.lower_a_ref, f32[256,256]{1,0:T(8,128)} %copy-done.3), custom_call_target="tpu_custom_call" | custom-call | tf_op jit(solution)/shard_map/pallas_call | solution.py:243
  295.6 12.5 %custom-call.9 = f32[128,128]{1,0:T(8,128)S(1)} custom-call(f32[128,128]{1,0:T(8,128)} %get-tuple-element.26), custom_call_target="Cholesky" | custom-call | tf_op jit(solution)/shard_map/cholesky/custom-call.1 | solution.py:246
  308.8 1.3 select_select_fusion.lower_c_ref
  310.1 4.8 %shard_map.73 = (f32[256,256]{1,0:T(8,128)}, f32[256,256]{1,0:T(8,128)}) custom-call(f32[128,128]{1,0:T(8,128)} %select_select_fusion.1.lower_a_ref, f32[128,128]{1,0:T(8,128)} %get-tuple-element.25.lower_b_ref, f32[128,128]{1,0:T(8,128)} %select_select_fusion.lower_c_ref, f32[128,128]{1,0:T(8,128)} %get-tuple-element.27.inv_a_ref), custom_call_target="tpu_custom_call" | custom-call | tf_op jit(solution)/shard_map/pallas_call | solution.py:248
  314.9 2.3 convolution_multiply_fusion
  317.2 9.0 %shard_map.74 = f32[768,2048]{1,0:T(8,128)} custom-call(f32[256,256]{1,0:T(8,128)} %get-tuple-element.28.inv_ref, f32[768,2048]{1,0:T(8,128)} %get-tuple-element.29.basis_ref), custom_call_target="tpu_custom_call" | custom-call | tf_op jit(solution)/shard_map/pallas_call | solution.py:139
  (43 shorter events, 8.3 us)
Async XLA Ops:
  0.6 17.7 %copy-start = (bf16[768,2048]{1,0:T(8,128)(2,1)S(1)}, bf16[768,2048]{1,0:T(8,128)(2,1)}, u32[]{:S(2)}) copy-start(bf16[768,2048]{1,0:T(8,128)(2,1)} %param.5) | copy-start | bytes 9437188
  1.8 0.8 copy-start.1
  6.8 25.8 %all-to-all-start.1 = ((s32[128,1,12]{2,1,0:T(1,128)}), s32[128,1,12]{2,1,0:T(1,128)S(1)}, u32[]{:S(2)}, u32[]{:S(2)}) async-start(s32[128,1,12]{2,1,0:T(1,128)} %bitcast.13), calls=%async_computation.1 | async-start | bytes 131072 | tf_op jit(solution)/shard_map/all_to_all | solution.py:291
  32.6 10.9 %copy-start.5 = (f32[2,9]{1,0:T(2,128)S(1)}, f32[2,9]{1,0:T(2,128)}, u32[]{:S(2)}) copy-start(f32[2,9]{1,0:T(2,128)} %taps_ref.1) | copy-start | bytes 220
  32.6 84.9 %all-to-all-start = ((bf16[128,12,16,128]{3,2,1,0:T(8,128)(2,1)}), bf16[128,12,16,128]{3,2,1,0:T(8,128)(2,1)}, u32[]{:S(2)}, u32[]{:S(2)}) async-start(bf16[128,12,16,128]{3,2,1,0:T(8,128)(2,1)} %bitcast.61), calls=%async_computation | async-start | bytes 12582912 | tf_op jit(solution)/shard_map/all_to_all | solution.py:284
  181.1 0.7 copy-start.2
  220.1 40.0 %copy-start.4 = (f32[256,256]{1,0:T(8,128)S(1)}, f32[256,256]{1,0:T(8,128)}, u32[]{:S(2)}) copy-start(f32[256,256]{1,0:T(8,128)} %get-tuple-element.31) | copy-start | bytes 786436
  254.8 16.2 %all-to-all-start.5 = ((f32[128,1,512]{2,1,0:T(1,128)}), f32[128,1,512]{2,1,0:T(1,128)}, u32[]{:S(2)}, u32[]{:S(2)}) async-start(f32[128,1,512]{2,1,0:T(1,128)} %broadcast_in_dim.21), calls=%async_computation.5 | async-start | bytes 524288 | tf_op jit(solution)/shard_map/all_to_all | solution.py:259
  276.0 0.7 copy-start.3

commit v3 on v2

--- a/solution.py
+++ b/solution.py
@@ -194,9 +194,15 @@
     return jnp.dot(a, b, precision=lax.Precision.HIGHEST, preferred_element_type=jnp.float32)
 
 
+def lower_part(square):
+    row = lax.broadcasted_iota(jnp.int32, square.shape, 0)
+    col = lax.broadcasted_iota(jnp.int32, square.shape, 1)
+    return jnp.where(row >= col, square, 0.0)
+
+
 def first_half_kernel(lower_a_ref, gram_ref, inv_a_ref, lower_b_ref, rest_ref):
     half = lower_a_ref.shape[0]
-    inv_a = doubling_inverse(lower_a_ref[...])
+    inv_a = doubling_inverse(lower_part(lower_a_ref[...]))
     inv_a_ref[...] = inv_a
     lower_b = nt_dot(gram_ref[half:, :half], inv_a)
     lower_b_ref[...] = lower_b
@@ -205,13 +211,14 @@
 
 def second_half_kernel(lower_a_ref, lower_b_ref, lower_c_ref, inv_a_ref, lower_ref, inverse_ref):
     half = lower_a_ref.shape[0]
-    inv_c = doubling_inverse(lower_c_ref[...])
+    lower_c = lower_part(lower_c_ref[...])
+    inv_c = doubling_inverse(lower_c)
     inv_a = inv_a_ref[...]
     zero = jnp.zeros((half, half), jnp.float32)
-    lower_ref[:half, :half] = lower_a_ref[...]
+    lower_ref[:half, :half] = lower_part(lower_a_ref[...])
     lower_ref[:half, half:] = zero
     lower_ref[half:, :half] = lower_b_ref[...]
-    lower_ref[half:, half:] = lower_c_ref[...]
+    lower_ref[half:, half:] = lower_c
     inverse_ref[:half, :half] = inv_a
     inverse_ref[:half, half:] = zero
     inverse_ref[half:, :half] = -nn_dot(inv_c, nn_dot(lower_b_ref[...], inv_a))
@@ -238,12 +245,12 @@
     size = gram.shape[0]
     half = size // 2
     gram = (gram + gram.T) / 2
-    lower_a = lax.linalg.cholesky(gram[:half, :half], symmetrize_input=False)
+    lower_a = lax.linalg.cholesky_p.bind(gram[:half, :half])
     square = jax.ShapeDtypeStruct((half, half), jnp.float32)
     inv_a, lower_b, rest = pl.pallas_call(
         first_half_kernel, out_shape=[square, square, square]
     )(lower_a, gram)
-    lower_c = lax.linalg.cholesky(rest, symmetrize_input=False)
+    lower_c = lax.linalg.cholesky_p.bind(rest)
     full = jax.ShapeDtypeStruct((size, size), jnp.float32)
     lower, inverse = pl.pallas_call(
         second_half_kernel, out_shape=[full, full]

time: 332 us -> 332 us (level)
    select_n x4 -> x0, other arithmetic: 5.16 us -> none  [the longest x2 2.6 us: factor_and_inverse(): lower_a = lax.linalg.cholesky(gram[:half, :half], symmetrize_input=False)]
    another operation x15 -> x19, other arithmetic: 51.5 us -> 56.7 us  [the longest x8 29 us: factor_and_inverse(): lower_c = lax.linalg.cholesky_p.bind(rest)]
where the time goes in v3:
time: 332 us; the launch traced here: 326 us
  waiting for transfers between devices  79.5 us (24%)
  other arithmetic  70.7 us (21%)
  Pallas kernels  65.3 us (20%)
  blocking collectives  49.2 us (15%)
  starting transfers between devices  27.4 us (8%)
  matrix products  19.3 us (6%)
  local copies, waits for them, and re-layouts  14 us (4%)
    all_to_all x1, waiting for transfers between devices, local(): lax.all_to_all(buffer.reshape(devices_all, capacity, PX, PZ), ('gx', 'gy'...  71.2 us
    all_to_all x2, blocking collectives, sum_over_devices(): rows = lax.all_to_all(rows, axes, 0, 0, tiled=True)  33.4 us
    another operation x8, other arithmetic, factor_and_inverse(): lower_c = lax.linalg.cholesky_p.bind(rest)  29 us
    another operation x8, other arithmetic, factor_and_inverse(): lower_a = lax.linalg.cholesky_p.bind(gram[:half, :half])  27.4 us
    all_to_all x1, blocking collectives, sum_over_devices(): total = lax.all_to_all(total, axes, 0, 0, tiled=True)  15.7 us
    pallas_call x1, Pallas kernels, filter_planes(): pl.pallas_call(filter_kernel, grid=(count // SNAP,), in_specs=[pl.BlockSp...  14.6 us
    pallas_call x1, Pallas kernels, basis_and_gram(): pl.pallas_call(basis_kernel, grid=(count // size,), in_specs=[pl.BlockSpe...  14.3 us
    all_to_all x1, starting transfers between devices, local(): lax.all_to_all(labels.reshape(devices_all, capacity), ('gx', 'gy'), split...  11.5 us
  transfers between devices with their start and end apart: 3, of which 2 were waited for; matrix products, arithmetic and copies ran while one was open for 4% of the time, Pallas kernels for 2%

profile of v3, /device:TPU:1, one launch (start us, length us, event | category | flops | bytes accessed | tf_op | source)
XLA Modules:
  0.0 326.4 jit_solution(3494419064253689895)
XLA Ops:
  0.6 0.9 copy.21
  1.8 0.8 copy-done.1
  2.6 1.1 add_add_fusion
  3.8 1.0 fusion.18
  6.1 0.7 sub.36
  6.8 11.5 %all-to-all-start.1 = ((s32[128,1,12]{2,1,0:T(1,128)}), s32[128,1,12]{2,1,0:T(1,128)S(1)}, u32[]{:S(2)}, u32[]{:S(2)}) async-start(s32[128,1,12]{2,1,0:T(1,128)} %bitcast.13), calls=%async_computation.1 | async-start | bytes 131072 | tf_op jit(solution)/shard_map/all_to_all | solution.py:298
  18.3 6.9 %convert_bitcast_fusion.planes_ref = bf16[16,1536,128]{2,1,0:T(8,128)(2,1)} fusion(s32[768]{0:T(1024)S(1)} %get-tuple-element.48, bf16[768,2048]{1,0:T(8,128)(2,1)S(1)} %copy-done), kind=kOutput, calls=%fused_computation.2 | convolution fusion | flops 4836163584 | bytes 9440256 | tf_op jit(solution)/shard_map/kr,rab->akb/dot_general | solution.py:282
  25.2 7.4 %shard_map.67 = bf16[1536,16,128]{2,1,0:T(8,128)(2,1)} custom-call(bf16[16,1536,128]{2,1,0:T(8,128)(2,1)} %convert_bitcast_fusion.planes_ref), custom_call_target="tpu_custom_call" | custom-call | tf_op jit(solution)/shard_map/pallas_call | solution.py:157
  32.6 10.6 %all-to-all-start = ((bf16[128,12,16,128]{3,2,1,0:T(8,128)(2,1)}), bf16[128,12,16,128]{3,2,1,0:T(8,128)(2,1)}, u32[]{:S(2)}, u32[]{:S(2)}) async-start(bf16[128,12,16,128]{3,2,1,0:T(8,128)(2,1)} %bitcast.61), calls=%async_computation | async-start | bytes 12582912 | tf_op jit(solution)/shard_map/all_to_all | solution.py:291
  46.4 71.2 %all-to-all-done = bf16[128,12,16,128]{3,2,1,0:T(8,128)(2,1)} async-done(((bf16[128,12,16,128]{3,2,1,0:T(8,128)(2,1)}), bf16[128,12,16,128]{3,2,1,0:T(8,128)(2,1)}, u32[]{:S(2)}, u32[]{:S(2)}) %all-to-all-start) | async-done | bytes 6291488 | tf_op jit(solution)/shard_map/all_to_all | solution.py:291
  117.6 9.5 %convert_bitcast_fusion.1.planes_ref = bf16[16,768,128]{2,1,0:T(8,128)(2,1)} fusion(s32[1536]{0:T(1024)S(1)} %fusion.30, bf16[1536,16,128]{2,1,0:T(8,128)(2,1)} %bitcast.12), kind=kOutput, calls=%fused_computation.10 | convolution fusion | flops 4834590720 | bytes 9443328 | tf_op jit(solution)/shard_map/tk,kab->atb/dot_general | solution.py:311
  127.1 14.6 %shard_map.68 = (f32[768,2048]{1,0:T(8,128)}, f32[256,256]{1,0:T(8,128)}) custom-call(f32[2,9]{1,0:T(2,128)} %taps_ref.1, bf16[128,384]{1,0:T(8,128)(2,1)} %pad_maximum_fusion.span_ref, bf16[16,768,128]{2,1,0:T(8,128)(2,1)} %convert_bitcast_fusion.1.planes_ref), custom_call_target="tpu_custom_call" | custom-call | tf_op jit(solution)/shard_map/pallas_call | solution.py:62
  141.7 1.2 all_to_all.35
  142.9 17.0 %all_to_all.43 = f32[128,1,512]{2,1,0:T(1,128)} all-to-all(f32[128,1,512]{2,1,0:T(1,128)S(1)} %all_to_all.35), channel_id=1, replica_groups=mesh['gx'=8,'gy'=16] {'gx','gy'}, dimensions={0} | all-to-all | bytes 524288 | tf_op jit(solution)/shard_map/all_to_all | solution.py:263
  159.9 1.2 reduce_sum.38
  161.2 15.7 %all_to_all.44 = f32[128,1,512]{2,1,0:T(1,128)S(1)} all-to-all(f32[128,1,512]{2,1,0:T(1,128)S(1)} %broadcast_in_dim.20), channel_id=1, replica_groups=mesh['gx'=8,'gy'=16] {'gx','gy'}, dimensions={0} | all-to-all | bytes 524288 | tf_op jit(solution)/shard_map/all_to_all | solution.py:266
  177.0 1.3 reduce.42
  178.3 1.0 reshape.176
  179.3 0.8 copy.28
  180.1 1.0 fusion.20.gram_ref
  181.8 11.7 %custom-call.6 = f32[128,128]{1,0:T(8,128)S(1)} custom-call(f32[128,128]{1,0:T(8,128)S(1)} %slice.23), custom_call_target="Cholesky" | custom-call | tf_op jit(solution)/shard_map/cholesky/custom-call.1 | solution.py:248
  193.6 0.7 compare_reduce_fusion.5
  194.3 1.3 broadcast_select_fusion.3.lower_a_ref
  195.6 5.2 %shard_map.69 = (f32[128,128]{1,0:T(8,128)}, f32[128,128]{1,0:T(8,128)}, f32[128,128]{1,0:T(8,128)}) custom-call(f32[128,128]{1,0:T(8,128)} %broadcast_select_fusion.3.lower_a_ref, f32[256,256]{1,0:T(8,128)} %copy-done.2), custom_call_target="tpu_custom_call" | custom-call | tf_op jit(solution)/shard_map/pallas_call | solution.py:250
  200.8 12.5 %custom-call.7 = f32[128,128]{1,0:T(8,128)S(1)} custom-call(f32[128,128]{1,0:T(8,128)} %get-tuple-element.20), custom_call_target="Cholesky" | custom-call | tf_op jit(solution)/shard_map/cholesky/custom-call.1 | solution.py:253
  214.0 1.3 broadcast_select_fusion.2.lower_c_ref
  215.3 4.8 %shard_map.70 = (f32[256,256]{1,0:T(8,128)}, f32[256,256]{1,0:T(8,128)}) custom-call(f32[128,128]{1,0:T(8,128)} %broadcast_select_fusion.3.lower_a_ref, f32[128,128]{1,0:T(8,128)} %get-tuple-element.19.lower_b_ref, f32[128,128]{1,0:T(8,128)} %broadcast_select_fusion.2.lower_c_ref, f32[128,128]{1,0:T(8,128)} %get-tuple-element.21.inv_a_ref), custom_call_target="tpu_custom_call" | custom-call | tf_op jit(solution)/shard_map/pallas_call | solution.py:255
  220.1 14.3 %shard_map.71 = (f32[768,2048]{1,0:T(8,128)}, f32[256,256]{1,0:T(8,128)}) custom-call(f32[256,256]{1,0:T(8,128)} %get-tuple-element.22.inv_ref, f32[768,2048]{1,0:T(8,128)} %get-tuple-element.23.matrix_ref), custom_call_target="tpu_custom_call" | custom-call | tf_op jit(solution)/shard_map/pallas_call | solution.py:106
  234.4 1.9 all_to_all.36
  236.3 16.4 %all_to_all.45 = f32[128,1,512]{2,1,0:T(1,128)} all-to-all(f32[128,1,512]{2,1,0:T(1,128)} %all_to_all.36), channel_id=1, replica_groups=mesh['gx'=8,'gy'=16] {'gx','gy'}, dimensions={0} | all-to-all | bytes 524288 | tf_op jit(solution)/shard_map/all_to_all | solution.py:263
  252.8 1.2 reduce_sum.39
  253.9 0.8 broadcast_in_dim.21
  254.8 5.3 %all-to-all-start.5 = ((f32[128,1,512]{2,1,0:T(1,128)}), f32[128,1,512]{2,1,0:T(1,128)}, u32[]{:S(2)}, u32[]{:S(2)}) async-start(f32[128,1,512]{2,1,0:T(1,128)} %broadcast_in_dim.21), calls=%async_computation.5 | async-start | bytes 524288 | tf_op jit(solution)/shard_map/all_to_all | solution.py:266
  260.1 0.7 multiply_bitcast_fusion
  260.8 1.8 copy.31
  262.6 8.4 %all-to-all-done.5 = f32[128,1,512]{2,1,0:T(1,128)} async-done(((f32[128,1,512]{2,1,0:T(1,128)}), f32[128,1,512]{2,1,0:T(1,128)}, u32[]{:S(2)}, u32[]{:S(2)}) %all-to-all-start.5) | async-done | bytes 262176 | tf_op jit(solution)/shard_map/all_to_all | solution.py:266
  270.9 2.3 reduce.43
  273.2 1.0 reshape.177
  274.2 0.8 copy.30
  275.1 1.0 fusion.19.gram_ref
  276.8 11.7 %custom-call.8 = f32[128,128]{1,0:T(8,128)S(1)} custom-call(f32[128,128]{1,0:T(8,128)S(1)} %slice.24), custom_call_target="Cholesky" | custom-call | tf_op jit(solution)/shard_map/cholesky/custom-call.1 | solution.py:248
  289.1 1.3 broadcast_select_fusion.1.lower_a_ref
  290.4 5.2 %shard_map.72 = (f32[128,128]{1,0:T(8,128)}, f32[128,128]{1,0:T(8,128)}, f32[128,128]{1,0:T(8,128)}) custom-call(f32[128,128]{1,0:T(8,128)} %broadcast_select_fusion.1.lower_a_ref, f32[256,256]{1,0:T(8,128)} %copy-done.3), custom_call_target="tpu_custom_call" | custom-call | tf_op jit(solution)/shard_map/pallas_call | solution.py:250
  295.6 12.5 %custom-call.9 = f32[128,128]{1,0:T(8,128)S(1)} custom-call(f32[128,128]{1,0:T(8,128)} %get-tuple-element.26), custom_call_target="Cholesky" | custom-call | tf_op jit(solution)/shard_map/cholesky/custom-call.1 | solution.py:253
  308.8 1.3 broadcast_select_fusion.lower_c_ref
  310.1 4.8 %shard_map.73 = (f32[256,256]{1,0:T(8,128)}, f32[256,256]{1,0:T(8,128)}) custom-call(f32[128,128]{1,0:T(8,128)} %broadcast_select_fusion.1.lower_a_ref, f32[128,128]{1,0:T(8,128)} %get-tuple-element.25.lower_b_ref, f32[128,128]{1,0:T(8,128)} %broadcast_select_fusion.lower_c_ref, f32[128,128]{1,0:T(8,128)} %get-tuple-element.27.inv_a_ref), custom_call_target="tpu_custom_call" | custom-call | tf_op jit(solution)/shard_map/pallas_call | solution.py:255
  314.9 2.3 convolution_multiply_fusion
  317.2 9.0 %shard_map.74 = f32[768,2048]{1,0:T(8,128)} custom-call(f32[256,256]{1,0:T(8,128)} %get-tuple-element.28.inv_ref, f32[768,2048]{1,0:T(8,128)} %get-tuple-element.29.basis_ref), custom_call_target="tpu_custom_call" | custom-call | tf_op jit(solution)/shard_map/pallas_call | solution.py:139
  (43 shorter events, 8.3 us)
Async XLA Ops:
  0.6 17.7 %copy-start = (bf16[768,2048]{1,0:T(8,128)(2,1)S(1)}, bf16[768,2048]{1,0:T(8,128)(2,1)}, u32[]{:S(2)}) copy-start(bf16[768,2048]{1,0:T(8,128)(2,1)} %param.5) | copy-start | bytes 9437188
  1.8 0.8 copy-start.1
  6.8 25.8 %all-to-all-start.1 = ((s32[128,1,12]{2,1,0:T(1,128)}), s32[128,1,12]{2,1,0:T(1,128)S(1)}, u32[]{:S(2)}, u32[]{:S(2)}) async-start(s32[128,1,12]{2,1,0:T(1,128)} %bitcast.13), calls=%async_computation.1 | async-start | bytes 131072 | tf_op jit(solution)/shard_map/all_to_all | solution.py:298
  32.6 10.9 %copy-start.5 = (f32[2,9]{1,0:T(2,128)S(1)}, f32[2,9]{1,0:T(2,128)}, u32[]{:S(2)}) copy-start(f32[2,9]{1,0:T(2,128)} %taps_ref.1) | copy-start | bytes 220
  32.6 84.9 %all-to-all-start = ((bf16[128,12,16,128]{3,2,1,0:T(8,128)(2,1)}), bf16[128,12,16,128]{3,2,1,0:T(8,128)(2,1)}, u32[]{:S(2)}, u32[]{:S(2)}) async-start(bf16[128,12,16,128]{3,2,1,0:T(8,128)(2,1)} %bitcast.61), calls=%async_computation | async-start | bytes 12582912 | tf_op jit(solution)/shard_map/all_to_all | solution.py:291
  181.1 0.7 copy-start.2
  220.1 40.0 %copy-start.4 = (f32[256,256]{1,0:T(8,128)S(1)}, f32[256,256]{1,0:T(8,128)}, u32[]{:S(2)}) copy-start(f32[256,256]{1,0:T(8,128)} %get-tuple-element.31) | copy-start | bytes 786436
  254.8 16.2 %all-to-all-start.5 = ((f32[128,1,512]{2,1,0:T(1,128)}), f32[128,1,512]{2,1,0:T(1,128)}, u32[]{:S(2)}, u32[]{:S(2)}) async-start(f32[128,1,512]{2,1,0:T(1,128)} %broadcast_in_dim.21), calls=%async_computation.5 | async-start | bytes 524288 | tf_op jit(solution)/shard_map/all_to_all | solution.py:266
  276.0 0.7 copy-start.3

commit v4 on v3

--- a/solution.py
+++ b/solution.py
@@ -80,24 +80,21 @@
 
 
 def basis_kernel(inv_ref, matrix_ref, basis_ref, gram_ref):
+    half = inv_ref.shape[0] // 2
+
     @pl.when(pl.program_id(0) == 0)
     def _():
         gram_ref[...] = jnp.zeros(gram_ref.shape, jnp.float32)
 
-    basis = jnp.dot(
-        inv_ref[...],
-        matrix_ref[...],
-        precision=lax.Precision.HIGHEST,
-        preferred_element_type=jnp.float32,
-    )
-    basis_ref[...] = basis
-    gram_ref[...] += lax.dot_general(
-        basis,
-        basis,
-        (((1,), (1,)), ((), ())),
-        precision=lax.Precision.HIGHEST,
-        preferred_element_type=jnp.float32,
-    )
+    top = nn_dot(inv_ref[:half, :half], matrix_ref[:half])
+    bottom = nn_dot(inv_ref[half:, :half], matrix_ref[:half]) + nn_dot(
+        inv_ref[half:, half:], matrix_ref[half:]
+    )
+    basis_ref[:half] = top
+    basis_ref[half:] = bottom
+    gram_ref[:half, :half] += nt_dot(top, top)
+    gram_ref[half:, :half] += nt_dot(bottom, top)
+    gram_ref[half:, half:] += nt_dot(bottom, bottom)
 
 
 def basis_and_gram(inverse, matrix):
@@ -122,15 +119,12 @@
 
 
 def modes_kernel(inv_ref, basis_ref, modes_ref, *, scale):
-    modes_ref[...] = (
-        jnp.dot(
-            inv_ref[...],
-            basis_ref[...],
-            precision=lax.Precision.HIGHEST,
-            preferred_element_type=jnp.float32,
-        )
-        * scale
-    )
+    half = inv_ref.shape[0] // 2
+    modes_ref[:half] = nn_dot(inv_ref[:half, :half], basis_ref[:half]) * scale
+    modes_ref[half:] = (
+        nn_dot(inv_ref[half:, :half], basis_ref[:half])
+        + nn_dot(inv_ref[half:, half:], basis_ref[half:])
+    ) * scale
 
 
 def modes_of(inverse, basis, scale):
@@ -206,7 +200,8 @@
     inv_a_ref[...] = inv_a
     lower_b = nt_dot(gram_ref[half:, :half], inv_a)
     lower_b_ref[...] = lower_b
-    rest_ref[...] = gram_ref[half:, half:] - nt_dot(lower_b, lower_b)
+    far = gram_ref[half:, half:]
+    rest_ref[...] = (far + far.T) / 2 - nt_dot(lower_b, lower_b)
 
 
 def second_half_kernel(lower_a_ref, lower_b_ref, lower_c_ref, inv_a_ref, lower_ref, inverse_ref):
@@ -244,8 +239,8 @@
 def factor_and_inverse(gram):
     size = gram.shape[0]
     half = size // 2
-    gram = (gram + gram.T) / 2
-    lower_a = lax.linalg.cholesky_p.bind(gram[:half, :half])
+    corner = gram[:half, :half]
+    lower_a = lax.linalg.cholesky_p.bind((corner + corner.T) / 2)
     square = jax.ShapeDtypeStruct((half, half), jnp.float32)
     inv_a, lower_b, rest = pl.pallas_call(
         first_half_kernel, out_shape=[square, square, square]

time: 332 us -> 333 us (level)
  Pallas kernels: 65.3 us -> 70.7 us
    pallas_call x1, Pallas kernels: 14.3 us -> 18.1 us  [basis_and_gram(): pl.pallas_call(basis_kernel, grid=(count // size,), in_specs=[pl.BlockSpe...]
where the time goes in v4:
time: 333 us; the launch traced here: 327 us
  waiting for transfers between devices  79.5 us (24%)
  Pallas kernels  70.7 us (21%)
  other arithmetic  68.8 us (21%)
  blocking collectives  49 us (15%)
  starting transfers between devices  27.4 us (8%)
  matrix products  19.5 us (6%)
  local copies, waits for them, and re-layouts  11.2 us (3%)
    all_to_all x1, waiting for transfers between devices, local(): lax.all_to_all(buffer.reshape(devices_all, capacity, PX, PZ), ('gx', 'gy'...  71.2 us
    all_to_all x2, blocking collectives, sum_over_devices(): rows = lax.all_to_all(rows, axes, 0, 0, tiled=True)  33.4 us
    another operation x8, other arithmetic, factor_and_inverse(): lower_c = lax.linalg.cholesky_p.bind(rest)  29 us
    another operation x8, other arithmetic, factor_and_inverse(): lower_a = lax.linalg.cholesky_p.bind((corner + corner.T) / 2)  27.4 us
    pallas_call x1, Pallas kernels, basis_and_gram(): pl.pallas_call(basis_kernel, grid=(count // size,), in_specs=[pl.BlockSpe...  18.1 us
    all_to_all x1, blocking collectives, sum_over_devices(): total = lax.all_to_all(total, axes, 0, 0, tiled=True)  15.5 us
    pallas_call x1, Pallas kernels, filter_planes(): pl.pallas_call(filter_kernel, grid=(count // SNAP,), in_specs=[pl.BlockSp...  14.6 us
    all_to_all x1, starting transfers between devices, local(): lax.all_to_all(labels.reshape(devices_all, capacity), ('gx', 'gy'), split...  11.5 us
  transfers between devices with their start and end apart: 3, of which 2 were waited for; matrix products, arithmetic and copies ran while one was open for 4% of the time, Pallas kernels for 2%

profile of v4, /device:TPU:1, one launch (start us, length us, event | category | flops | bytes accessed | tf_op | source)
XLA Modules:
  0.0 327.1 jit_solution(15022184414702361963)
XLA Ops:
  0.6 0.9 copy.23
  1.8 0.8 copy-done.1
  2.6 1.1 add_add_fusion
  3.8 1.0 fusion.18
  4.8 0.7 multiply_add_fusion
  6.1 0.7 sub.36
  6.8 11.5 %all-to-all-start.1 = ((s32[128,1,12]{2,1,0:T(1,128)}), s32[128,1,12]{2,1,0:T(1,128)S(1)}, u32[]{:S(2)}, u32[]{:S(2)}) async-start(s32[128,1,12]{2,1,0:T(1,128)} %bitcast.13), calls=%async_computation.1 | async-start | bytes 131072 | tf_op jit(solution)/shard_map/all_to_all | solution.py:293
  18.3 6.9 %convert_bitcast_fusion.planes_ref = bf16[16,1536,128]{2,1,0:T(8,128)(2,1)} fusion(s32[768]{0:T(1024)S(1)} %get-tuple-element.48, bf16[768,2048]{1,0:T(8,128)(2,1)S(1)} %copy-done), kind=kOutput, calls=%fused_computation.2 | convolution fusion | flops 4836163584 | bytes 9440256 | tf_op jit(solution)/shard_map/kr,rab->akb/dot_general | solution.py:277
  25.2 7.4 %shard_map.67 = bf16[1536,16,128]{2,1,0:T(8,128)(2,1)} custom-call(bf16[16,1536,128]{2,1,0:T(8,128)(2,1)} %convert_bitcast_fusion.planes_ref), custom_call_target="tpu_custom_call" | custom-call | tf_op jit(solution)/shard_map/pallas_call | solution.py:151
  32.7 10.5 %all-to-all-start = ((bf16[128,12,16,128]{3,2,1,0:T(8,128)(2,1)}), bf16[128,12,16,128]{3,2,1,0:T(8,128)(2,1)}, u32[]{:S(2)}, u32[]{:S(2)}) async-start(bf16[128,12,16,128]{3,2,1,0:T(8,128)(2,1)} %bitcast.61), calls=%async_computation | async-start | bytes 12582912 | tf_op jit(solution)/shard_map/all_to_all | solution.py:286
  44.2 0.7 pad_maximum_fusion.span_ref
  46.4 71.2 %all-to-all-done = bf16[128,12,16,128]{3,2,1,0:T(8,128)(2,1)} async-done(((bf16[128,12,16,128]{3,2,1,0:T(8,128)(2,1)}), bf16[128,12,16,128]{3,2,1,0:T(8,128)(2,1)}, u32[]{:S(2)}, u32[]{:S(2)}) %all-to-all-start) | async-done | bytes 6291488 | tf_op jit(solution)/shard_map/all_to_all | solution.py:286
  117.6 9.5 %convert_bitcast_fusion.1.planes_ref = bf16[16,768,128]{2,1,0:T(8,128)(2,1)} fusion(s32[1536]{0:T(1024)S(1)} %fusion.30, bf16[1536,16,128]{2,1,0:T(8,128)(2,1)} %bitcast.12), kind=kOutput, calls=%fused_computation.10 | convolution fusion | flops 4834590720 | bytes 9443328 | tf_op jit(solution)/shard_map/tk,kab->atb/dot_general | solution.py:306
  127.1 14.6 %shard_map.68 = (f32[768,2048]{1,0:T(8,128)}, f32[256,256]{1,0:T(8,128)}) custom-call(f32[2,9]{1,0:T(2,128)} %taps_ref.1, bf16[128,384]{1,0:T(8,128)(2,1)} %pad_maximum_fusion.span_ref, bf16[16,768,128]{2,1,0:T(8,128)(2,1)} %convert_bitcast_fusion.1.planes_ref), custom_call_target="tpu_custom_call" | custom-call | tf_op jit(solution)/shard_map/pallas_call | solution.py:62
  141.7 1.2 all_to_all.35
  142.9 17.0 %all_to_all.43 = f32[128,1,512]{2,1,0:T(1,128)} all-to-all(f32[128,1,512]{2,1,0:T(1,128)S(1)} %all_to_all.35), channel_id=1, replica_groups=mesh['gx'=8,'gy'=16] {'gx','gy'}, dimensions={0} | all-to-all | bytes 524288 | tf_op jit(solution)/shard_map/all_to_all | solution.py:258
  159.9 1.2 reduce_sum.38
  161.2 15.5 %all_to_all.44 = f32[128,1,512]{2,1,0:T(1,128)S(1)} all-to-all(f32[128,1,512]{2,1,0:T(1,128)S(1)} %broadcast_in_dim.20), channel_id=1, replica_groups=mesh['gx'=8,'gy'=16] {'gx','gy'}, dimensions={0} | all-to-all | bytes 524288 | tf_op jit(solution)/shard_map/all_to_all | solution.py:261
  176.8 1.3 reduce.42
  178.1 1.0 reshape.176.gram_ref
  179.2 11.7 %custom-call.6 = f32[128,128]{1,0:T(8,128)S(1)} custom-call(f32[128,128]{1,0:T(8,128)S(1)} %fusion.22), custom_call_target="Cholesky" | custom-call | tf_op jit(solution)/shard_map/cholesky/custom-call.1 | solution.py:243
  191.0 0.7 compare_reduce_fusion.5
  191.7 1.3 broadcast_select_fusion.3.lower_a_ref
  193.0 5.2 %shard_map.69 = (f32[128,128]{1,0:T(8,128)}, f32[128,128]{1,0:T(8,128)}, f32[128,128]{1,0:T(8,128)}) custom-call(f32[128,128]{1,0:T(8,128)} %broadcast_select_fusion.3.lower_a_ref, f32[256,256]{1,0:T(8,128)} %copy-done.2), custom_call_target="tpu_custom_call" | custom-call | tf_op jit(solution)/shard_map/pallas_call | solution.py:245
  198.2 12.5 %custom-call.7 = f32[128,128]{1,0:T(8,128)S(1)} custom-call(f32[128,128]{1,0:T(8,128)} %get-tuple-element.20), custom_call_target="Cholesky" | custom-call | tf_op jit(solution)/shard_map/cholesky/custom-call.1 | solution.py:248
  210.8 0.6 compare_reduce_fusion.4
  211.4 1.3 broadcast_select_fusion.2.lower_c_ref
  212.7 4.8 %shard_map.70 = (f32[256,256]{1,0:T(8,128)}, f32[256,256]{1,0:T(8,128)}) custom-call(f32[128,128]{1,0:T(8,128)} %broadcast_select_fusion.3.lower_a_ref, f32[128,128]{1,0:T(8,128)} %get-tuple-element.19.lower_b_ref, f32[128,128]{1,0:T(8,128)} %broadcast_select_fusion.2.lower_c_ref, f32[128,128]{1,0:T(8,128)} %get-tuple-element.21.inv_a_ref), custom_call_target="tpu_custom_call" | custom-call | tf_op jit(solution)/shard_map/pallas_call | solution.py:250
  217.5 18.1 %shard_map.71 = (f32[768,2048]{1,0:T(8,128)}, f32[256,256]{1,0:T(8,128)}) custom-call(f32[256,256]{1,0:T(8,128)} %get-tuple-element.22.inv_ref, f32[768,2048]{1,0:T(8,128)} %get-tuple-element.23.matrix_ref), custom_call_target="tpu_custom_call" | custom-call | tf_op jit(solution)/shard_map/pallas_call | solution.py:103
  235.6 1.9 all_to_all.36
  237.5 16.4 %all_to_all.45 = f32[128,1,512]{2,1,0:T(1,128)} all-to-all(f32[128,1,512]{2,1,0:T(1,128)} %all_to_all.36), channel_id=1, replica_groups=mesh['gx'=8,'gy'=16] {'gx','gy'}, dimensions={0} | all-to-all | bytes 524288 | tf_op jit(solution)/shard_map/all_to_all | solution.py:258
  253.9 1.2 reduce_sum.39
  255.1 0.8 broadcast_in_dim.21
  255.9 5.3 %all-to-all-start.5 = ((f32[128,1,512]{2,1,0:T(1,128)}), f32[128,1,512]{2,1,0:T(1,128)}, u32[]{:S(2)}, u32[]{:S(2)}) async-start(f32[128,1,512]{2,1,0:T(1,128)} %broadcast_in_dim.21), calls=%async_computation.5 | async-start | bytes 524288 | tf_op jit(solution)/shard_map/all_to_all | solution.py:261
  261.2 0.7 multiply_bitcast_fusion
  262.0 1.8 copy.34
  263.8 8.4 %all-to-all-done.5 = f32[128,1,512]{2,1,0:T(1,128)} async-done(((f32[128,1,512]{2,1,0:T(1,128)}), f32[128,1,512]{2,1,0:T(1,128)}, u32[]{:S(2)}, u32[]{:S(2)}) %all-to-all-start.5) | async-done | bytes 262176 | tf_op jit(solution)/shard_map/all_to_all | solution.py:261
  272.1 2.3 reduce.43
  274.4 1.0 reshape.177.gram_ref
  275.5 11.7 %custom-call.8 = f32[128,128]{1,0:T(8,128)S(1)} custom-call(f32[128,128]{1,0:T(8,128)S(1)} %fusion.21), custom_call_target="Cholesky" | custom-call | tf_op jit(solution)/shard_map/cholesky/custom-call.1 | solution.py:243
  287.3 0.6 compare_reduce_fusion.3
  287.9 1.3 broadcast_select_fusion.1.lower_a_ref
  289.2 5.2 %shard_map.72 = (f32[128,128]{1,0:T(8,128)}, f32[128,128]{1,0:T(8,128)}, f32[128,128]{1,0:T(8,128)}) custom-call(f32[128,128]{1,0:T(8,128)} %broadcast_select_fusion.1.lower_a_ref, f32[256,256]{1,0:T(8,128)} %copy-done.3), custom_call_target="tpu_custom_call" | custom-call | tf_op jit(solution)/shard_map/pallas_call | solution.py:245
  294.4 12.5 %custom-call.9 = f32[128,128]{1,0:T(8,128)S(1)} custom-call(f32[128,128]{1,0:T(8,128)} %get-tuple-element.26), custom_call_target="Cholesky" | custom-call | tf_op jit(solution)/shard_map/cholesky/custom-call.1 | solution.py:248
  307.6 1.3 broadcast_select_fusion.lower_c_ref
  308.9 4.8 %shard_map.73 = (f32[256,256]{1,0:T(8,128)}, f32[256,256]{1,0:T(8,128)}) custom-call(f32[128,128]{1,0:T(8,128)} %broadcast_select_fusion.1.lower_a_ref, f32[128,128]{1,0:T(8,128)} %get-tuple-element.25.lower_b_ref, f32[128,128]{1,0:T(8,128)} %broadcast_select_fusion.lower_c_ref, f32[128,128]{1,0:T(8,128)} %get-tuple-element.27.inv_a_ref), custom_call_target="tpu_custom_call" | custom-call | tf_op jit(solution)/shard_map/pallas_call | solution.py:250
  313.6 2.5 convolution_multiply_fusion
  316.2 10.7 %shard_map.74 = f32[768,2048]{1,0:T(8,128)} custom-call(f32[256,256]{1,0:T(8,128)} %get-tuple-element.28.inv_ref, f32[768,2048]{1,0:T(8,128)} %get-tuple-element.29.basis_ref), custom_call_target="tpu_custom_call" | custom-call | tf_op jit(solution)/shard_map/pallas_call | solution.py:133
  (43 shorter events, 4.5 us)
Async XLA Ops:
  0.6 17.7 %copy-start = (bf16[768,2048]{1,0:T(8,128)(2,1)S(1)}, bf16[768,2048]{1,0:T(8,128)(2,1)}, u32[]{:S(2)}) copy-start(bf16[768,2048]{1,0:T(8,128)(2,1)} %param.5) | copy-start | bytes 9437188
  1.8 0.8 copy-start.1
  6.8 25.8 %all-to-all-start.1 = ((s32[128,1,12]{2,1,0:T(1,128)}), s32[128,1,12]{2,1,0:T(1,128)S(1)}, u32[]{:S(2)}, u32[]{:S(2)}) async-start(s32[128,1,12]{2,1,0:T(1,128)} %bitcast.13), calls=%async_computation.1 | async-start | bytes 131072 | tf_op jit(solution)/shard_map/all_to_all | solution.py:293
  32.7 10.9 %copy-start.5 = (f32[2,9]{1,0:T(2,128)S(1)}, f32[2,9]{1,0:T(2,128)}, u32[]{:S(2)}) copy-start(f32[2,9]{1,0:T(2,128)} %taps_ref.1) | copy-start | bytes 220
  32.7 84.9 %all-to-all-start = ((bf16[128,12,16,128]{3,2,1,0:T(8,128)(2,1)}), bf16[128,12,16,128]{3,2,1,0:T(8,128)(2,1)}, u32[]{:S(2)}, u32[]{:S(2)}) async-start(bf16[128,12,16,128]{3,2,1,0:T(8,128)(2,1)} %bitcast.61), calls=%async_computation | async-start | bytes 12582912 | tf_op jit(solution)/shard_map/all_to_all | solution.py:286
  179.1 13.9 %copy-start.2 = (f32[256,256]{1,0:T(8,128)}, f32[256,256]{1,0:T(8,128)S(1)}, u32[]{:S(2)}) copy-start(f32[256,256]{1,0:T(8,128)S(1)} %reshape.176.gram_ref) | copy-start | bytes 786436
  217.5 43.7 %copy-start.4 = (f32[256,256]{1,0:T(8,128)S(1)}, f32[256,256]{1,0:T(8,128)}, u32[]{:S(2)}) copy-start(f32[256,256]{1,0:T(8,128)} %get-tuple-element.31) | copy-start | bytes 786436
  255.9 16.2 %all-to-all-start.5 = ((f32[128,1,512]{2,1,0:T(1,128)}), f32[128,1,512]{2,1,0:T(1,128)}, u32[]{:S(2)}, u32[]{:S(2)}) async-start(f32[128,1,512]{2,1,0:T(1,128)} %broadcast_in_dim.21), calls=%async_computation.5 | async-start | bytes 524288 | tf_op jit(solution)/shard_map/all_to_all | solution.py:261
  275.4 13.8 %copy-start.3 = (f32[256,256]{1,0:T(8,128)}, f32[256,256]{1,0:T(8,128)S(1)}, u32[]{:S(2)}) copy-start(f32[256,256]{1,0:T(8,128)S(1)} %reshape.177.gram_ref) | copy-start | bytes 786436

commit v5 on v2

--- a/solution.py
+++ b/solution.py
@@ -146,6 +146,33 @@
         out_specs=pl.BlockSpec((size, width), lambda i: (i, 0)),
         out_shape=jax.ShapeDtypeStruct((count, width), jnp.float32),
     )(inverse, basis)
+
+
+def route_kernel(slot_ref, records_ref, buffer_ref, planes_ref):
+    rows = buffer_ref.shape[0]
+    first = pl.program_id(0) * rows
+    places = first + lax.broadcasted_iota(jnp.int32, (rows, slot_ref.shape[1]), 0)
+    pick = (slot_ref[...] == places).astype(jnp.bfloat16)
+    for x in range(PX):
+        planes_ref[x] = jnp.dot(
+            pick, records_ref[:, x * PZ : (x + 1) * PZ], preferred_element_type=jnp.float32
+        ).astype(jnp.bfloat16)
+    buffer_ref[...] = pltpu.einshape("akb->kab", planes_ref[...])
+
+
+def route_records(slot, records, slots, rows=256):
+    count, width = records.shape
+    return pl.pallas_call(
+        route_kernel,
+        grid=(slots // rows,),
+        in_specs=[
+            pl.BlockSpec((1, count), lambda i: (0, 0)),
+            pl.BlockSpec((count, width), lambda i: (0, 0)),
+        ],
+        out_specs=pl.BlockSpec((rows, PX, PZ), lambda i: (i, 0, 0)),
+        out_shape=jax.ShapeDtypeStruct((slots, PX, PZ), jnp.bfloat16),
+        scratch_shapes=[pltpu.VMEM((PX, rows, PZ), jnp.bfloat16)],
+    )(slot.reshape(1, count), records)
 
 
 def swap_kernel(planes_ref, records_ref):
@@ -272,13 +299,7 @@
     slot = record_owner * capacity + position
     places = jnp.arange(devices_all * capacity, dtype=jnp.int32)
     pick = slot[None, :] == places[:, None]
-    buffer = jnp.einsum(
-        "kr,rab->akb",
-        pick.astype(jnp.bfloat16),
-        records.reshape(rec_count, PX, PZ),
-        preferred_element_type=jnp.float32,
-    ).astype(jnp.bfloat16)
-    buffer = planes_to_records(buffer)
+    buffer = route_records(slot, records, devices_all * capacity)
     labels = jnp.sum(jnp.where(pick, record_field[None, :] + 1, 0), axis=1) - 1
     arrived, arrived_labels = (
         lax.all_to_all(

time: 332 us -> 316 us (0.952)
  other arithmetic: 70.7 us -> 62.6 us
  Pallas kernels: 65.2 us -> 72.6 us
  matrix products: 19.3 us -> 12.3 us
  local copies, waits for them, and re-layouts: 14 us -> 7.32 us
    pallas_call x1, Pallas kernels: 7.43 us -> 14.8 us  [route_records(): pl.pallas_call(route_kernel, grid=(slots // rows,), in_specs=[pl.BlockSpe...]
    dot_general x1 -> x0, matrix products: 6.9 us -> none  [local(): jnp.einsum('kr,rab->akb', pick.astype(jnp.bfloat16), records.reshape(rec_...]
    reshape x4, local copies, waits for them, and re-layouts: 3.66 us -> 0.34 us  [sum_over_devices(): return total.reshape(part.shape)]
  transfers between devices with their start and end apart: 3 -> 3, of which waited for: 2 -> 2; matrix products, arithmetic and copies ran while one was open for 4% -> 1% of each run, Pallas kernels for 2% -> 5%
where the time goes in v5:
time: 316 us; the launch traced here: 312 us
  waiting for transfers between devices  81.4 us (26%)
  Pallas kernels  72.6 us (23%)
  other arithmetic  62.6 us (20%)
  blocking collectives  47.9 us (15%)
  starting transfers between devices  26.4 us (8%)
  matrix products  12.3 us (4%)
  local copies, waits for them, and re-layouts  7.32 us (2%)
    all_to_all x1, waiting for transfers between devices, local(): lax.all_to_all(buffer.reshape(devices_all, capacity, PX, PZ), ('gx', 'gy'...  71.2 us
    all_to_all x2, blocking collectives, sum_over_devices(): rows = lax.all_to_all(rows, axes, 0, 0, tiled=True)  32.2 us
    another operation x6, other arithmetic, factor_and_inverse(): lower_c = lax.linalg.cholesky(rest, symmetrize_input=False)  26.4 us
    another operation x6, other arithmetic, factor_and_inverse(): lower_a = lax.linalg.cholesky(gram[:half, :half], symmetrize_input=False)  24.8 us
    all_to_all x1, blocking collectives, sum_over_devices(): total = lax.all_to_all(total, axes, 0, 0, tiled=True)  15.7 us
    pallas_call x1, Pallas kernels, route_records(): pl.pallas_call(route_kernel, grid=(slots // rows,), in_specs=[pl.BlockSpe...  14.8 us
    pallas_call x1, Pallas kernels, filter_planes(): pl.pallas_call(filter_kernel, grid=(count // SNAP,), in_specs=[pl.BlockSp...  14.6 us
    pallas_call x1, Pallas kernels, basis_and_gram(): pl.pallas_call(basis_kernel, grid=(count // size,), in_specs=[pl.BlockSpe...  14.4 us
  transfers between devices with their start and end apart: 3, of which 2 were waited for; matrix products, arithmetic and copies ran while one was open for 1% of the time, Pallas kernels for 5%

profile of v5, /device:TPU:1, one launch (start us, length us, event | category | flops | bytes accessed | tf_op | source)
XLA Modules:
  0.0 311.8 jit_solution(16535260806770041972)
XLA Ops:
  0.6 0.8 copy.29
  1.8 1.0 fusion.13
  2.8 0.7 multiply_add_fusion
  3.5 0.6 select_reduce_fusion
  4.1 0.7 sub.36
  4.8 11.5 %all-to-all-start.1 = ((s32[128,1,12]{2,1,0:T(1,128)}), s32[128,1,12]{2,1,0:T(1,128)S(1)}, u32[]{:S(2)}, u32[]{:S(2)}) async-start(s32[128,1,12]{2,1,0:T(1,128)} %bitcast.11), calls=%async_computation.1 | async-start | bytes 131072 | tf_op jit(solution)/shard_map/all_to_all | solution.py:312
  16.3 0.6 reshape.173.slot_ref
  16.9 14.8 %shard_map.67 = bf16[1536,16,128]{2,1,0:T(8,128)(2,1)} custom-call(s32[1,768]{1,0:T(1,128)} %reshape.173.slot_ref, bf16[768,2048]{1,0:T(8,128)(2,1)} %records_ref.1), custom_call_target="tpu_custom_call" | custom-call | tf_op jit(solution)/shard_map/pallas_call | solution.py:165
  31.7 10.6 %all-to-all-start = ((bf16[128,12,16,128]{3,2,1,0:T(8,128)(2,1)}), bf16[128,12,16,128]{3,2,1,0:T(8,128)(2,1)}, u32[]{:S(2)}, u32[]{:S(2)}) async-start(bf16[128,12,16,128]{3,2,1,0:T(8,128)(2,1)} %bitcast.49), calls=%async_computation | async-start | bytes 12582912 | tf_op jit(solution)/shard_map/all_to_all | solution.py:305
  42.3 0.2 iota_compare_fusion.2
  42.6 0.5 fusion.9
  43.3 0.7 pad_maximum_fusion.span_ref
  43.9 0.5 divide_reduce_fusion
  44.6 0.5 compare_reduce_fusion
  45.4 71.2 %all-to-all-done = bf16[128,12,16,128]{3,2,1,0:T(8,128)(2,1)} async-done(((bf16[128,12,16,128]{3,2,1,0:T(8,128)(2,1)}), bf16[128,12,16,128]{3,2,1,0:T(8,128)(2,1)}, u32[]{:S(2)}, u32[]{:S(2)}) %all-to-all-start) | async-done | bytes 6291488 | tf_op jit(solution)/shard_map/all_to_all | solution.py:305
  116.6 9.5 %convert_bitcast_fusion.planes_ref = bf16[16,768,128]{2,1,0:T(8,128)(2,1)} fusion(s32[1536]{0:T(1024)S(1)} %fusion.25, bf16[1536,16,128]{2,1,0:T(8,128)(2,1)} %bitcast.10), kind=kOutput, calls=%fused_computation.6 | convolution fusion | flops 4834590720 | bytes 9443328 | tf_op jit(solution)/shard_map/tk,kab->atb/dot_general | solution.py:325
  126.1 14.6 %shard_map.68 = (f32[768,2048]{1,0:T(8,128)}, f32[256,256]{1,0:T(8,128)}) custom-call(f32[2,9]{1,0:T(2,128)} %taps_ref.1, bf16[128,384]{1,0:T(8,128)(2,1)} %pad_maximum_fusion.span_ref, bf16[16,768,128]{2,1,0:T(8,128)(2,1)} %convert_bitcast_fusion.planes_ref), custom_call_target="tpu_custom_call" | custom-call | tf_op jit(solution)/shard_map/pallas_call | solution.py:62
  140.7 1.2 all_to_all.35
  141.9 16.9 %all_to_all.43 = f32[128,1,512]{2,1,0:T(1,128)S(1)} all-to-all(f32[128,1,512]{2,1,0:T(1,128)S(1)} %all_to_all.35), channel_id=1, replica_groups=mesh['gx'=8,'gy'=16] {'gx','gy'}, dimensions={0} | all-to-all | bytes 524288 | tf_op jit(solution)/shard_map/all_to_all | solution.py:283
  158.9 0.2 reduce_sum.38
  159.2 15.7 %all_to_all.44 = f32[128,1,512]{2,1,0:T(1,128)S(1)} all-to-all(f32[128,1,512]{2,1,0:T(1,128)S(1)} %broadcast_in_dim.20), channel_id=1, replica_groups=mesh['gx'=8,'gy'=16] {'gx','gy'}, dimensions={0} | all-to-all | bytes 524288 | tf_op jit(solution)/shard_map/all_to_all | solution.py:286
  174.9 0.6 reduce.42
  175.8 11.7 %custom-call.6 = f32[128,128]{1,0:T(8,128)S(1)} custom-call(f32[128,128]{1,0:T(8,128)S(1)} %slice.23), custom_call_target="Cholesky" | custom-call | tf_op jit(solution)/shard_map/cholesky/custom-call.1 | solution.py:268
  187.6 0.6 compare_reduce_fusion.5
  188.2 1.3 select_select_fusion.3.lower_a_ref
  189.5 5.2 %shard_map.69 = (f32[128,128]{1,0:T(8,128)}, f32[128,128]{1,0:T(8,128)}, f32[128,128]{1,0:T(8,128)}) custom-call(f32[128,128]{1,0:T(8,128)} %select_select_fusion.3.lower_a_ref, f32[256,256]{1,0:T(8,128)} %copy-done), custom_call_target="tpu_custom_call" | custom-call | tf_op jit(solution)/shard_map/pallas_call | solution.py:270
  194.7 12.5 %custom-call.7 = f32[128,128]{1,0:T(8,128)S(1)} custom-call(f32[128,128]{1,0:T(8,128)} %get-tuple-element.20), custom_call_target="Cholesky" | custom-call | tf_op jit(solution)/shard_map/cholesky/custom-call.1 | solution.py:273
  207.3 0.6 compare_reduce_fusion.4
  207.9 1.3 select_select_fusion.2.lower_c_ref
  209.2 4.8 %shard_map.70 = (f32[256,256]{1,0:T(8,128)}, f32[256,256]{1,0:T(8,128)}) custom-call(f32[128,128]{1,0:T(8,128)} %select_select_fusion.3.lower_a_ref, f32[128,128]{1,0:T(8,128)} %get-tuple-element.19.lower_b_ref, f32[128,128]{1,0:T(8,128)} %select_select_fusion.2.lower_c_ref, f32[128,128]{1,0:T(8,128)} %get-tuple-element.21.inv_a_ref), custom_call_target="tpu_custom_call" | custom-call | tf_op jit(solution)/shard_map/pallas_call | solution.py:275
  213.9 14.4 %shard_map.71 = (f32[768,2048]{1,0:T(8,128)}, f32[256,256]{1,0:T(8,128)}) custom-call(f32[256,256]{1,0:T(8,128)} %get-tuple-element.22.inv_ref, f32[768,2048]{1,0:T(8,128)} %get-tuple-element.23.matrix_ref), custom_call_target="tpu_custom_call" | custom-call | tf_op jit(solution)/shard_map/pallas_call | solution.py:106
  228.3 1.2 all_to_all.36
  229.5 15.3 %all_to_all.45 = f32[128,1,512]{2,1,0:T(1,128)S(1)} all-to-all(f32[128,1,512]{2,1,0:T(1,128)S(1)} %all_to_all.36), channel_id=1, replica_groups=mesh['gx'=8,'gy'=16] {'gx','gy'}, dimensions={0} | all-to-all | bytes 524288 | tf_op jit(solution)/shard_map/all_to_all | solution.py:283
  245.0 0.8 broadcast_in_dim.21
  245.8 4.4 %all-to-all-start.5 = ((f32[128,1,512]{2,1,0:T(1,128)}), f32[128,1,512]{2,1,0:T(1,128)S(1)}, u32[]{:S(2)}, u32[]{:S(2)}) async-start(f32[128,1,512]{2,1,0:T(1,128)} %broadcast_in_dim.21), calls=%async_computation.5 | async-start | bytes 524288 | tf_op jit(solution)/shard_map/all_to_all | solution.py:286
  250.3 0.8 copy.38
  251.1 10.2 %all-to-all-done.5 = f32[128,1,512]{2,1,0:T(1,128)S(1)} async-done(((f32[128,1,512]{2,1,0:T(1,128)}), f32[128,1,512]{2,1,0:T(1,128)S(1)}, u32[]{:S(2)}, u32[]{:S(2)}) %all-to-all-start.5) | async-done | bytes 262176 | tf_op jit(solution)/shard_map/all_to_all | solution.py:286
  261.3 0.6 reduce.43
  262.2 11.7 %custom-call.8 = f32[128,128]{1,0:T(8,128)S(1)} custom-call(f32[128,128]{1,0:T(8,128)S(1)} %slice.24), custom_call_target="Cholesky" | custom-call | tf_op jit(solution)/shard_map/cholesky/custom-call.1 | solution.py:268
  274.0 0.6 compare_reduce_fusion.3
  274.6 1.3 select_select_fusion.1.lower_a_ref
  275.9 5.2 %shard_map.72 = (f32[128,128]{1,0:T(8,128)}, f32[128,128]{1,0:T(8,128)}, f32[128,128]{1,0:T(8,128)}) custom-call(f32[128,128]{1,0:T(8,128)} %select_select_fusion.1.lower_a_ref, f32[256,256]{1,0:T(8,128)} %copy-done.1), custom_call_target="tpu_custom_call" | custom-call | tf_op jit(solution)/shard_map/pallas_call | solution.py:270
  281.1 12.5 %custom-call.9 = f32[128,128]{1,0:T(8,128)S(1)} custom-call(f32[128,128]{1,0:T(8,128)} %get-tuple-element.26), custom_call_target="Cholesky" | custom-call | tf_op jit(solution)/shard_map/cholesky/custom-call.1 | solution.py:273
  293.7 0.6 compare_reduce_fusion.2
  294.3 1.3 select_select_fusion.lower_c_ref
  295.6 4.8 %shard_map.73 = (f32[256,256]{1,0:T(8,128)}, f32[256,256]{1,0:T(8,128)}) custom-call(f32[128,128]{1,0:T(8,128)} %select_select_fusion.1.lower_a_ref, f32[128,128]{1,0:T(8,128)} %get-tuple-element.25.lower_b_ref, f32[128,128]{1,0:T(8,128)} %select_select_fusion.lower_c_ref, f32[128,128]{1,0:T(8,128)} %get-tuple-element.27.inv_a_ref), custom_call_target="tpu_custom_call" | custom-call | tf_op jit(solution)/shard_map/pallas_call | solution.py:275
  300.3 2.2 convolution_multiply_fusion
  302.6 9.0 %shard_map.74 = f32[768,2048]{1,0:T(8,128)} custom-call(f32[256,256]{1,0:T(8,128)} %get-tuple-element.28.inv_ref, f32[768,2048]{1,0:T(8,128)} %get-tuple-element.29.basis_ref), custom_call_target="tpu_custom_call" | custom-call | tf_op jit(solution)/shard_map/pallas_call | solution.py:139
  (39 shorter events, 2.0 us)
Async XLA Ops:
  4.8 26.9 %all-to-all-start.1 = ((s32[128,1,12]{2,1,0:T(1,128)}), s32[128,1,12]{2,1,0:T(1,128)S(1)}, u32[]{:S(2)}, u32[]{:S(2)}) async-start(s32[128,1,12]{2,1,0:T(1,128)} %bitcast.11), calls=%async_computation.1 | async-start | bytes 131072 | tf_op jit(solution)/shard_map/all_to_all | solution.py:312
  31.7 10.9 %copy-start.3 = (f32[2,9]{1,0:T(2,128)S(1)}, f32[2,9]{1,0:T(2,128)}, u32[]{:S(2)}) copy-start(f32[2,9]{1,0:T(2,128)} %taps_ref.1) | copy-start | bytes 220
  31.7 84.9 %all-to-all-start = ((bf16[128,12,16,128]{3,2,1,0:T(8,128)(2,1)}), bf16[128,12,16,128]{3,2,1,0:T(8,128)(2,1)}, u32[]{:S(2)}, u32[]{:S(2)}) async-start(bf16[128,12,16,128]{3,2,1,0:T(8,128)(2,1)} %bitcast.49), calls=%async_computation | async-start | bytes 12582912 | tf_op jit(solution)/shard_map/all_to_all | solution.py:305
  175.8 13.7 %copy-start = (f32[256,256]{1,0:T(8,128)}, f32[256,256]{1,0:T(8,128)S(1)}, u32[]{:S(2)}) copy-start(f32[256,256]{1,0:T(8,128)S(1)} %fusion.15.gram_ref) | copy-start | bytes 786436
  213.9 36.3 %copy-start.2 = (f32[256,256]{1,0:T(8,128)S(1)}, f32[256,256]{1,0:T(8,128)}, u32[]{:S(2)}) copy-start(f32[256,256]{1,0:T(8,128)} %get-tuple-element.31) | copy-start | bytes 786436
  245.8 15.5 %all-to-all-start.5 = ((f32[128,1,512]{2,1,0:T(1,128)}), f32[128,1,512]{2,1,0:T(1,128)S(1)}, u32[]{:S(2)}, u32[]{:S(2)}) async-start(f32[128,1,512]{2,1,0:T(1,128)} %broadcast_in_dim.21), calls=%async_computation.5 | async-start | bytes 524288 | tf_op jit(solution)/shard_map/all_to_all | solution.py:286
  262.2 13.7 %copy-start.1 = (f32[256,256]{1,0:T(8,128)}, f32[256,256]{1,0:T(8,128)S(1)}, u32[]{:S(2)}) copy-start(f32[256,256]{1,0:T(8,128)S(1)} %fusion.14.gram_ref) | copy-start | bytes 786436

commit v6 on v5

--- a/solution.py
+++ b/solution.py
@@ -160,7 +160,7 @@
     buffer_ref[...] = pltpu.einshape("akb->kab", planes_ref[...])
 
 
-def route_records(slot, records, slots, rows=256):
+def route_records(slot, records, slots, rows=512):
     count, width = records.shape
     return pl.pallas_call(
         route_kernel,

time: 316 us -> 316 us (level)
  transfers between devices with their start and end apart: 3 -> 3, of which waited for: 2 -> 2; matrix products, arithmetic and copies ran while one was open for 1% -> 1% of each run, Pallas kernels for 5% -> 4%
where the time goes in v6:
time: 316 us; the launch traced here: 311 us
  waiting for transfers between devices  81.4 us (26%)
  Pallas kernels  71.4 us (23%)
  other arithmetic  62.6 us (20%)
  blocking collectives  47.9 us (15%)
  starting transfers between devices  26.4 us (8%)
  matrix products  12.3 us (4%)
  local copies, waits for them, and re-layouts  7.32 us (2%)
    all_to_all x1, waiting for transfers between devices, local(): lax.all_to_all(buffer.reshape(devices_all, capacity, PX, PZ), ('gx', 'gy'...  71.2 us
    all_to_all x2, blocking collectives, sum_over_devices(): rows = lax.all_to_all(rows, axes, 0, 0, tiled=True)  32.2 us
    another operation x6, other arithmetic, factor_and_inverse(): lower_c = lax.linalg.cholesky(rest, symmetrize_input=False)  26.4 us
    another operation x6, other arithmetic, factor_and_inverse(): lower_a = lax.linalg.cholesky(gram[:half, :half], symmetrize_input=False)  24.8 us
    all_to_all x1, blocking collectives, sum_over_devices(): total = lax.all_to_all(total, axes, 0, 0, tiled=True)  15.7 us
    pallas_call x1, Pallas kernels, filter_planes(): pl.pallas_call(filter_kernel, grid=(count // SNAP,), in_specs=[pl.BlockSp...  14.6 us
    pallas_call x1, Pallas kernels, basis_and_gram(): pl.pallas_call(basis_kernel, grid=(count // size,), in_specs=[pl.BlockSpe...  14.4 us
    pallas_call x1, Pallas kernels, route_records(): pl.pallas_call(route_kernel, grid=(slots // rows,), in_specs=[pl.BlockSpe...  13.5 us
  transfers between devices with their start and end apart: 3, of which 2 were waited for; matrix products, arithmetic and copies ran while one was open for 1% of the time, Pallas kernels for 4%

profile of v6, /device:TPU:1, one launch (start us, length us, event | category | flops | bytes accessed | tf_op | source)
XLA Modules:
  0.0 310.5 jit_solution(4039166126144821362)
XLA Ops:
  0.6 0.8 copy.29
  1.8 1.0 fusion.13
  2.8 0.7 multiply_add_fusion
  3.5 0.6 select_reduce_fusion
  4.1 0.7 sub.36
  4.8 11.5 %all-to-all-start.1 = ((s32[128,1,12]{2,1,0:T(1,128)}), s32[128,1,12]{2,1,0:T(1,128)S(1)}, u32[]{:S(2)}, u32[]{:S(2)}) async-start(s32[128,1,12]{2,1,0:T(1,128)} %bitcast.11), calls=%async_computation.1 | async-start | bytes 131072 | tf_op jit(solution)/shard_map/all_to_all | solution.py:312
  16.3 0.6 reshape.173.slot_ref
  16.9 13.5 %shard_map.67 = bf16[1536,16,128]{2,1,0:T(8,128)(2,1)} custom-call(s32[1,768]{1,0:T(1,128)} %reshape.173.slot_ref, bf16[768,2048]{1,0:T(8,128)(2,1)} %records_ref.1), custom_call_target="tpu_custom_call" | custom-call | tf_op jit(solution)/shard_map/pallas_call | solution.py:165
  30.4 10.6 %all-to-all-start = ((bf16[128,12,16,128]{3,2,1,0:T(8,128)(2,1)}), bf16[128,12,16,128]{3,2,1,0:T(8,128)(2,1)}, u32[]{:S(2)}, u32[]{:S(2)}) async-start(bf16[128,12,16,128]{3,2,1,0:T(8,128)(2,1)} %bitcast.49), calls=%async_computation | async-start | bytes 12582912 | tf_op jit(solution)/shard_map/all_to_all | solution.py:305
  41.1 0.2 iota_compare_fusion.2
  41.3 0.5 fusion.9
  42.0 0.7 pad_maximum_fusion.span_ref
  42.7 0.5 divide_reduce_fusion
  43.4 0.5 compare_reduce_fusion
  44.2 71.2 %all-to-all-done = bf16[128,12,16,128]{3,2,1,0:T(8,128)(2,1)} async-done(((bf16[128,12,16,128]{3,2,1,0:T(8,128)(2,1)}), bf16[128,12,16,128]{3,2,1,0:T(8,128)(2,1)}, u32[]{:S(2)}, u32[]{:S(2)}) %all-to-all-start) | async-done | bytes 6291488 | tf_op jit(solution)/shard_map/all_to_all | solution.py:305
  115.4 9.5 %convert_bitcast_fusion.planes_ref = bf16[16,768,128]{2,1,0:T(8,128)(2,1)} fusion(s32[1536]{0:T(1024)S(1)} %fusion.25, bf16[1536,16,128]{2,1,0:T(8,128)(2,1)} %bitcast.10), kind=kOutput, calls=%fused_computation.6 | convolution fusion | flops 4834590720 | bytes 9443328 | tf_op jit(solution)/shard_map/tk,kab->atb/dot_general | solution.py:325
  124.9 14.6 %shard_map.68 = (f32[768,2048]{1,0:T(8,128)}, f32[256,256]{1,0:T(8,128)}) custom-call(f32[2,9]{1,0:T(2,128)} %taps_ref.1, bf16[128,384]{1,0:T(8,128)(2,1)} %pad_maximum_fusion.span_ref, bf16[16,768,128]{2,1,0:T(8,128)(2,1)} %convert_bitcast_fusion.planes_ref), custom_call_target="tpu_custom_call" | custom-call | tf_op jit(solution)/shard_map/pallas_call | solution.py:62
  139.4 1.2 all_to_all.35
  140.7 16.9 %all_to_all.43 = f32[128,1,512]{2,1,0:T(1,128)S(1)} all-to-all(f32[128,1,512]{2,1,0:T(1,128)S(1)} %all_to_all.35), channel_id=1, replica_groups=mesh['gx'=8,'gy'=16] {'gx','gy'}, dimensions={0} | all-to-all | bytes 524288 | tf_op jit(solution)/shard_map/all_to_all | solution.py:283
  157.6 0.2 reduce_sum.38
  158.0 15.7 %all_to_all.44 = f32[128,1,512]{2,1,0:T(1,128)S(1)} all-to-all(f32[128,1,512]{2,1,0:T(1,128)S(1)} %broadcast_in_dim.20), channel_id=1, replica_groups=mesh['gx'=8,'gy'=16] {'gx','gy'}, dimensions={0} | all-to-all | bytes 524288 | tf_op jit(solution)/shard_map/all_to_all | solution.py:286
  173.7 0.6 reduce.42
  174.6 11.7 %custom-call.6 = f32[128,128]{1,0:T(8,128)S(1)} custom-call(f32[128,128]{1,0:T(8,128)S(1)} %slice.23), custom_call_target="Cholesky" | custom-call | tf_op jit(solution)/shard_map/cholesky/custom-call.1 | solution.py:268
  186.3 0.6 compare_reduce_fusion.5
  187.0 1.3 select_select_fusion.3.lower_a_ref
  188.2 5.2 %shard_map.69 = (f32[128,128]{1,0:T(8,128)}, f32[128,128]{1,0:T(8,128)}, f32[128,128]{1,0:T(8,128)}) custom-call(f32[128,128]{1,0:T(8,128)} %select_select_fusion.3.lower_a_ref, f32[256,256]{1,0:T(8,128)} %copy-done), custom_call_target="tpu_custom_call" | custom-call | tf_op jit(solution)/shard_map/pallas_call | solution.py:270
  193.4 12.5 %custom-call.7 = f32[128,128]{1,0:T(8,128)S(1)} custom-call(f32[128,128]{1,0:T(8,128)} %get-tuple-element.20), custom_call_target="Cholesky" | custom-call | tf_op jit(solution)/shard_map/cholesky/custom-call.1 | solution.py:273
  206.0 0.6 compare_reduce_fusion.4
  206.6 1.3 select_select_fusion.2.lower_c_ref
  207.9 4.8 %shard_map.70 = (f32[256,256]{1,0:T(8,128)}, f32[256,256]{1,0:T(8,128)}) custom-call(f32[128,128]{1,0:T(8,128)} %select_select_fusion.3.lower_a_ref, f32[128,128]{1,0:T(8,128)} %get-tuple-element.19.lower_b_ref, f32[128,128]{1,0:T(8,128)} %select_select_fusion.2.lower_c_ref, f32[128,128]{1,0:T(8,128)} %get-tuple-element.21.inv_a_ref), custom_call_target="tpu_custom_call" | custom-call | tf_op jit(solution)/shard_map/pallas_call | solution.py:275
  212.7 14.4 %shard_map.71 = (f32[768,2048]{1,0:T(8,128)}, f32[256,256]{1,0:T(8,128)}) custom-call(f32[256,256]{1,0:T(8,128)} %get-tuple-element.22.inv_ref, f32[768,2048]{1,0:T(8,128)} %get-tuple-element.23.matrix_ref), custom_call_target="tpu_custom_call" | custom-call | tf_op jit(solution)/shard_map/pallas_call | solution.py:106
  227.1 1.2 all_to_all.36
  228.3 15.3 %all_to_all.45 = f32[128,1,512]{2,1,0:T(1,128)S(1)} all-to-all(f32[128,1,512]{2,1,0:T(1,128)S(1)} %all_to_all.36), channel_id=1, replica_groups=mesh['gx'=8,'gy'=16] {'gx','gy'}, dimensions={0} | all-to-all | bytes 524288 | tf_op jit(solution)/shard_map/all_to_all | solution.py:283
  243.8 0.8 broadcast_in_dim.21
  244.6 4.4 %all-to-all-start.5 = ((f32[128,1,512]{2,1,0:T(1,128)}), f32[128,1,512]{2,1,0:T(1,128)S(1)}, u32[]{:S(2)}, u32[]{:S(2)}) async-start(f32[128,1,512]{2,1,0:T(1,128)} %broadcast_in_dim.21), calls=%async_computation.5 | async-start | bytes 524288 | tf_op jit(solution)/shard_map/all_to_all | solution.py:286
  249.0 0.8 copy.38
  249.9 10.2 %all-to-all-done.5 = f32[128,1,512]{2,1,0:T(1,128)S(1)} async-done(((f32[128,1,512]{2,1,0:T(1,128)}), f32[128,1,512]{2,1,0:T(1,128)S(1)}, u32[]{:S(2)}, u32[]{:S(2)}) %all-to-all-start.5) | async-done | bytes 262176 | tf_op jit(solution)/shard_map/all_to_all | solution.py:286
  260.1 0.6 reduce.43
  261.0 11.7 %custom-call.8 = f32[128,128]{1,0:T(8,128)S(1)} custom-call(f32[128,128]{1,0:T(8,128)S(1)} %slice.24), custom_call_target="Cholesky" | custom-call | tf_op jit(solution)/shard_map/cholesky/custom-call.1 | solution.py:268
  272.7 0.6 compare_reduce_fusion.3
  273.4 1.3 select_select_fusion.1.lower_a_ref
  274.6 5.2 %shard_map.72 = (f32[128,128]{1,0:T(8,128)}, f32[128,128]{1,0:T(8,128)}, f32[128,128]{1,0:T(8,128)}) custom-call(f32[128,128]{1,0:T(8,128)} %select_select_fusion.1.lower_a_ref, f32[256,256]{1,0:T(8,128)} %copy-done.1), custom_call_target="tpu_custom_call" | custom-call | tf_op jit(solution)/shard_map/pallas_call | solution.py:270
  279.8 12.5 %custom-call.9 = f32[128,128]{1,0:T(8,128)S(1)} custom-call(f32[128,128]{1,0:T(8,128)} %get-tuple-element.26), custom_call_target="Cholesky" | custom-call | tf_op jit(solution)/shard_map/cholesky/custom-call.1 | solution.py:273
  292.4 0.6 compare_reduce_fusion.2
  293.0 1.3 select_select_fusion.lower_c_ref
  294.3 4.8 %shard_map.73 = (f32[256,256]{1,0:T(8,128)}, f32[256,256]{1,0:T(8,128)}) custom-call(f32[128,128]{1,0:T(8,128)} %select_select_fusion.1.lower_a_ref, f32[128,128]{1,0:T(8,128)} %get-tuple-element.25.lower_b_ref, f32[128,128]{1,0:T(8,128)} %select_select_fusion.lower_c_ref, f32[128,128]{1,0:T(8,128)} %get-tuple-element.27.inv_a_ref), custom_call_target="tpu_custom_call" | custom-call | tf_op jit(solution)/shard_map/pallas_call | solution.py:275
  299.1 2.2 convolution_multiply_fusion
  301.3 9.0 %shard_map.74 = f32[768,2048]{1,0:T(8,128)} custom-call(f32[256,256]{1,0:T(8,128)} %get-tuple-element.28.inv_ref, f32[768,2048]{1,0:T(8,128)} %get-tuple-element.29.basis_ref), custom_call_target="tpu_custom_call" | custom-call | tf_op jit(solution)/shard_map/pallas_call | solution.py:139
  (39 shorter events, 2.0 us)
Async XLA Ops:
  4.8 25.6 %all-to-all-start.1 = ((s32[128,1,12]{2,1,0:T(1,128)}), s32[128,1,12]{2,1,0:T(1,128)S(1)}, u32[]{:S(2)}, u32[]{:S(2)}) async-start(s32[128,1,12]{2,1,0:T(1,128)} %bitcast.11), calls=%async_computation.1 | async-start | bytes 131072 | tf_op jit(solution)/shard_map/all_to_all | solution.py:312
  30.4 10.9 %copy-start.3 = (f32[2,9]{1,0:T(2,128)S(1)}, f32[2,9]{1,0:T(2,128)}, u32[]{:S(2)}) copy-start(f32[2,9]{1,0:T(2,128)} %taps_ref.1) | copy-start | bytes 220
  30.4 84.9 %all-to-all-start = ((bf16[128,12,16,128]{3,2,1,0:T(8,128)(2,1)}), bf16[128,12,16,128]{3,2,1,0:T(8,128)(2,1)}, u32[]{:S(2)}, u32[]{:S(2)}) async-start(bf16[128,12,16,128]{3,2,1,0:T(8,128)(2,1)} %bitcast.49), calls=%async_computation | async-start | bytes 12582912 | tf_op jit(solution)/shard_map/all_to_all | solution.py:305
  174.5 13.7 %copy-start = (f32[256,256]{1,0:T(8,128)}, f32[256,256]{1,0:T(8,128)S(1)}, u32[]{:S(2)}) copy-start(f32[256,256]{1,0:T(8,128)S(1)} %fusion.15.gram_ref) | copy-start | bytes 786436
  212.7 36.3 %copy-start.2 = (f32[256,256]{1,0:T(8,128)S(1)}, f32[256,256]{1,0:T(8,128)}, u32[]{:S(2)}) copy-start(f32[256,256]{1,0:T(8,128)} %get-tuple-element.31) | copy-start | bytes 786436
  244.6 15.5 %all-to-all-start.5 = ((f32[128,1,512]{2,1,0:T(1,128)}), f32[128,1,512]{2,1,0:T(1,128)S(1)}, u32[]{:S(2)}, u32[]{:S(2)}) async-start(f32[128,1,512]{2,1,0:T(1,128)} %broadcast_in_dim.21), calls=%async_computation.5 | async-start | bytes 524288 | tf_op jit(solution)/shard_map/all_to_all | solution.py:286
  260.9 13.7 %copy-start.1 = (f32[256,256]{1,0:T(8,128)}, f32[256,256]{1,0:T(8,128)S(1)}, u32[]{:S(2)}) copy-start(f32[256,256]{1,0:T(8,128)S(1)} %fusion.14.gram_ref) | copy-start | bytes 786436

commit v7 on v6

--- a/solution.py
+++ b/solution.py
@@ -245,6 +245,13 @@
     inverse_ref[half:, half:] = inv_c
 
 
+def last_half_kernel(
+    lower_a_ref, lower_b_ref, lower_c_ref, inv_a_ref, first_ref, lower_ref, inverse_ref, r_ref, *, scale
+):
+    second_half_kernel(lower_a_ref, lower_b_ref, lower_c_ref, inv_a_ref, lower_ref, inverse_ref)
+    r_ref[...] = jnp.transpose(nn_dot(first_ref[...], lower_ref[...])) / scale
+
+
 def gram_of(matrix):
     return lax.dot_general(
         matrix,
@@ -261,7 +268,7 @@
     )
 
 
-def factor_and_inverse(gram):
+def factor_and_inverse(gram, first=None, scale=1.0):
     size = gram.shape[0]
     half = size // 2
     gram = (gram + gram.T) / 2
@@ -272,10 +279,13 @@
     )(lower_a, gram)
     lower_c = lax.linalg.cholesky(rest, symmetrize_input=False)
     full = jax.ShapeDtypeStruct((size, size), jnp.float32)
-    lower, inverse = pl.pallas_call(
-        second_half_kernel, out_shape=[full, full]
-    )(lower_a, lower_b, lower_c, inv_a)
-    return lower, inverse
+    if first is None:
+        return pl.pallas_call(second_half_kernel, out_shape=[full, full])(
+            lower_a, lower_b, lower_c, inv_a
+        )
+    return pl.pallas_call(
+        functools.partial(last_half_kernel, scale=scale), out_shape=[full, full, full]
+    )(lower_a, lower_b, lower_c, inv_a, first)
 
 
 def sum_over_devices(part, axes, devices_all):
@@ -328,18 +338,11 @@
     fields, gram_one = filter_planes(planes, filter_taps)
     lower_one, inv_one = factor_and_inverse(sum_over_devices(gram_one, ("gx", "gy"), devices_all))
     basis_one, gram_two = basis_and_gram(inv_one, fields)
-    lower_two, inv_two = factor_and_inverse(sum_over_devices(gram_two, ("gx", "gy"), devices_all))
     scale = math.sqrt(3.0 * cells * devices_all)
+    lower_two, inv_two, r_factor = factor_and_inverse(
+        sum_over_devices(gram_two, ("gx", "gy"), devices_all), lower_one, scale
+    )
     modes = modes_of(inv_two, basis_one, scale).reshape(3, SNAP, cells)
-    r_factor = (
-        jnp.dot(
-            lower_two.T,
-            lower_one.T,
-            precision=lax.Precision.HIGHEST,
-            preferred_element_type=jnp.float32,
-        )
-        / scale
-    )
     first_factor = lower_one.T / scale
     return (modes.transpose(1, 0, 2), r_factor, first_factor)
 

time: 316 us -> 314 us (level)
    pallas_call x0 -> x1, Pallas kernels: none -> 5.23 us  [factor_and_inverse(): pl.pallas_call(functools.partial(last_half_kernel, scale=scale), out_shap...]
    pallas_call x2 -> x1, Pallas kernels: 9.52 us -> 4.76 us  [factor_and_inverse(): pl.pallas_call(second_half_kernel, out_shape=[full, full])]
where the time goes in v7:
time: 314 us; the launch traced here: 309 us
  waiting for transfers between devices  81.4 us (26%)
  Pallas kernels  71.8 us (23%)
  other arithmetic  62.8 us (20%)
  blocking collectives  47.9 us (15%)
  starting transfers between devices  26.4 us (8%)
  matrix products  10.1 us (3%)
  local copies, waits for them, and re-layouts  7.32 us (2%)
    all_to_all x1, waiting for transfers between devices, local(): lax.all_to_all(buffer.reshape(devices_all, capacity, PX, PZ), ('gx', 'gy'...  71.2 us
    all_to_all x2, blocking collectives, sum_over_devices(): rows = lax.all_to_all(rows, axes, 0, 0, tiled=True)  32.2 us
    another operation x6, other arithmetic, factor_and_inverse(): lower_c = lax.linalg.cholesky(rest, symmetrize_input=False)  26.4 us
    another operation x6, other arithmetic, factor_and_inverse(): lower_a = lax.linalg.cholesky(gram[:half, :half], symmetrize_input=False)  24.9 us
    all_to_all x1, blocking collectives, sum_over_devices(): total = lax.all_to_all(total, axes, 0, 0, tiled=True)  15.7 us
    pallas_call x1, Pallas kernels, filter_planes(): pl.pallas_call(filter_kernel, grid=(count // SNAP,), in_specs=[pl.BlockSp...  14.6 us
    pallas_call x1, Pallas kernels, basis_and_gram(): pl.pallas_call(basis_kernel, grid=(count // size,), in_specs=[pl.BlockSpe...  14.3 us
    pallas_call x1, Pallas kernels, route_records(): pl.pallas_call(route_kernel, grid=(slots // rows,), in_specs=[pl.BlockSpe...  13.5 us
  transfers between devices with their start and end apart: 3, of which 2 were waited for; matrix products, arithmetic and copies ran while one was open for 1% of the time, Pallas kernels for 4%

profile of v7, /device:TPU:1, one launch (start us, length us, event | category | flops | bytes accessed | tf_op | source)
XLA Modules:
  0.0 308.8 jit_solution(1067401483827704706)
XLA Ops:
  0.6 0.8 copy.29
  1.8 1.0 fusion.13
  2.8 0.7 multiply_add_fusion
  3.5 0.6 select_reduce_fusion
  4.1 0.7 sub.36
  4.8 11.5 %all-to-all-start.1 = ((s32[128,1,12]{2,1,0:T(1,128)}), s32[128,1,12]{2,1,0:T(1,128)S(1)}, u32[]{:S(2)}, u32[]{:S(2)}) async-start(s32[128,1,12]{2,1,0:T(1,128)} %bitcast.11), calls=%async_computation.1 | async-start | bytes 131072 | tf_op jit(solution)/shard_map/all_to_all | solution.py:322
  16.3 0.6 reshape.173.slot_ref
  16.9 13.5 %shard_map.67 = bf16[1536,16,128]{2,1,0:T(8,128)(2,1)} custom-call(s32[1,768]{1,0:T(1,128)} %reshape.173.slot_ref, bf16[768,2048]{1,0:T(8,128)(2,1)} %records_ref.1), custom_call_target="tpu_custom_call" | custom-call | tf_op jit(solution)/shard_map/pallas_call | solution.py:165
  30.4 10.6 %all-to-all-start = ((bf16[128,12,16,128]{3,2,1,0:T(8,128)(2,1)}), bf16[128,12,16,128]{3,2,1,0:T(8,128)(2,1)}, u32[]{:S(2)}, u32[]{:S(2)}) async-start(bf16[128,12,16,128]{3,2,1,0:T(8,128)(2,1)} %bitcast.47), calls=%async_computation | async-start | bytes 12582912 | tf_op jit(solution)/shard_map/all_to_all | solution.py:315
  41.1 0.2 iota_compare_fusion.2
  41.3 0.5 fusion.9
  42.0 0.7 pad_maximum_fusion.span_ref
  42.7 0.5 compare_reduce_fusion
  43.4 0.5 divide_reduce_fusion
  44.2 71.2 %all-to-all-done = bf16[128,12,16,128]{3,2,1,0:T(8,128)(2,1)} async-done(((bf16[128,12,16,128]{3,2,1,0:T(8,128)(2,1)}), bf16[128,12,16,128]{3,2,1,0:T(8,128)(2,1)}, u32[]{:S(2)}, u32[]{:S(2)}) %all-to-all-start) | async-done | bytes 6291488 | tf_op jit(solution)/shard_map/all_to_all | solution.py:315
  115.4 9.5 %convert_bitcast_fusion.planes_ref = bf16[16,768,128]{2,1,0:T(8,128)(2,1)} fusion(s32[1536]{0:T(1024)S(1)} %fusion.25, bf16[1536,16,128]{2,1,0:T(8,128)(2,1)} %bitcast.10), kind=kOutput, calls=%fused_computation.6 | convolution fusion | flops 4834590720 | bytes 9443328 | tf_op jit(solution)/shard_map/tk,kab->atb/dot_general | solution.py:335
  124.9 14.6 %shard_map.68 = (f32[768,2048]{1,0:T(8,128)}, f32[256,256]{1,0:T(8,128)}) custom-call(f32[2,9]{1,0:T(2,128)} %taps_ref.1, bf16[128,384]{1,0:T(8,128)(2,1)} %pad_maximum_fusion.span_ref, bf16[16,768,128]{2,1,0:T(8,128)(2,1)} %convert_bitcast_fusion.planes_ref), custom_call_target="tpu_custom_call" | custom-call | tf_op jit(solution)/shard_map/pallas_call | solution.py:62
  139.4 1.2 all_to_all.35
  140.7 16.9 %all_to_all.43 = f32[128,1,512]{2,1,0:T(1,128)S(1)} all-to-all(f32[128,1,512]{2,1,0:T(1,128)S(1)} %all_to_all.35), channel_id=1, replica_groups=mesh['gx'=8,'gy'=16] {'gx','gy'}, dimensions={0} | all-to-all | bytes 524288 | tf_op jit(solution)/shard_map/all_to_all | solution.py:293
  157.6 0.2 reduce_sum.38
  158.0 15.7 %all_to_all.44 = f32[128,1,512]{2,1,0:T(1,128)S(1)} all-to-all(f32[128,1,512]{2,1,0:T(1,128)S(1)} %broadcast_in_dim.20), channel_id=1, replica_groups=mesh['gx'=8,'gy'=16] {'gx','gy'}, dimensions={0} | all-to-all | bytes 524288 | tf_op jit(solution)/shard_map/all_to_all | solution.py:296
  173.7 0.6 reduce.42
  174.6 11.7 %custom-call.6 = f32[128,128]{1,0:T(8,128)S(1)} custom-call(f32[128,128]{1,0:T(8,128)S(1)} %slice.23), custom_call_target="Cholesky" | custom-call | tf_op jit(solution)/shard_map/cholesky/custom-call.1 | solution.py:275
  186.3 0.7 compare_reduce_fusion.5
  187.0 1.3 select_select_fusion.3.lower_a_ref
  188.4 5.2 %shard_map.69 = (f32[128,128]{1,0:T(8,128)}, f32[128,128]{1,0:T(8,128)}, f32[128,128]{1,0:T(8,128)}) custom-call(f32[128,128]{1,0:T(8,128)} %select_select_fusion.3.lower_a_ref, f32[256,256]{1,0:T(8,128)} %copy-done), custom_call_target="tpu_custom_call" | custom-call | tf_op jit(solution)/shard_map/pallas_call | solution.py:277
  193.5 12.5 %custom-call.7 = f32[128,128]{1,0:T(8,128)S(1)} custom-call(f32[128,128]{1,0:T(8,128)} %get-tuple-element.20), custom_call_target="Cholesky" | custom-call | tf_op jit(solution)/shard_map/cholesky/custom-call.1 | solution.py:280
  206.1 0.6 compare_reduce_fusion.4
  206.8 1.3 select_select_fusion.2.lower_c_ref
  208.0 4.8 %shard_map.70 = (f32[256,256]{1,0:T(8,128)}, f32[256,256]{1,0:T(8,128)}) custom-call(f32[128,128]{1,0:T(8,128)} %select_select_fusion.3.lower_a_ref, f32[128,128]{1,0:T(8,128)} %get-tuple-element.19.lower_b_ref, f32[128,128]{1,0:T(8,128)} %select_select_fusion.2.lower_c_ref, f32[128,128]{1,0:T(8,128)} %get-tuple-element.21.inv_a_ref), custom_call_target="tpu_custom_call" | custom-call | tf_op jit(solution)/shard_map/pallas_call | solution.py:283
  212.8 14.3 %shard_map.71 = (f32[768,2048]{1,0:T(8,128)}, f32[256,256]{1,0:T(8,128)}) custom-call(f32[256,256]{1,0:T(8,128)} %get-tuple-element.22.inv_ref, f32[768,2048]{1,0:T(8,128)} %get-tuple-element.23.matrix_ref), custom_call_target="tpu_custom_call" | custom-call | tf_op jit(solution)/shard_map/pallas_call | solution.py:106
  227.1 1.2 all_to_all.36
  228.4 15.3 %all_to_all.45 = f32[128,1,512]{2,1,0:T(1,128)S(1)} all-to-all(f32[128,1,512]{2,1,0:T(1,128)S(1)} %all_to_all.36), channel_id=1, replica_groups=mesh['gx'=8,'gy'=16] {'gx','gy'}, dimensions={0} | all-to-all | bytes 524288 | tf_op jit(solution)/shard_map/all_to_all | solution.py:293
  243.6 0.2 reduce_sum.39
  243.8 0.8 broadcast_in_dim.21
  244.7 4.4 %all-to-all-start.5 = ((f32[128,1,512]{2,1,0:T(1,128)}), f32[128,1,512]{2,1,0:T(1,128)S(1)}, u32[]{:S(2)}, u32[]{:S(2)}) async-start(f32[128,1,512]{2,1,0:T(1,128)} %broadcast_in_dim.21), calls=%async_computation.5 | async-start | bytes 524288 | tf_op jit(solution)/shard_map/all_to_all | solution.py:296
  249.1 0.8 copy.38
  249.9 10.2 %all-to-all-done.5 = f32[128,1,512]{2,1,0:T(1,128)S(1)} async-done(((f32[128,1,512]{2,1,0:T(1,128)}), f32[128,1,512]{2,1,0:T(1,128)S(1)}, u32[]{:S(2)}, u32[]{:S(2)}) %all-to-all-start.5) | async-done | bytes 262176 | tf_op jit(solution)/shard_map/all_to_all | solution.py:296
  260.2 0.6 reduce.43
  261.1 11.7 %custom-call.8 = f32[128,128]{1,0:T(8,128)S(1)} custom-call(f32[128,128]{1,0:T(8,128)S(1)} %slice.24), custom_call_target="Cholesky" | custom-call | tf_op jit(solution)/shard_map/cholesky/custom-call.1 | solution.py:275
  272.8 0.6 compare_reduce_fusion.3
  273.5 1.3 select_select_fusion.1.lower_a_ref
  274.7 5.2 %shard_map.72 = (f32[128,128]{1,0:T(8,128)}, f32[128,128]{1,0:T(8,128)}, f32[128,128]{1,0:T(8,128)}) custom-call(f32[128,128]{1,0:T(8,128)} %select_select_fusion.1.lower_a_ref, f32[256,256]{1,0:T(8,128)} %copy-done.1), custom_call_target="tpu_custom_call" | custom-call | tf_op jit(solution)/shard_map/pallas_call | solution.py:277
  279.9 12.5 %custom-call.9 = f32[128,128]{1,0:T(8,128)S(1)} custom-call(f32[128,128]{1,0:T(8,128)} %get-tuple-element.26), custom_call_target="Cholesky" | custom-call | tf_op jit(solution)/shard_map/cholesky/custom-call.1 | solution.py:280
  292.5 0.6 compare_reduce_fusion.2
  293.1 1.3 select_select_fusion.lower_c_ref
  294.4 5.2 %shard_map.73 = (f32[256,256]{1,0:T(8,128)}, f32[256,256]{1,0:T(8,128)}, f32[256,256]{1,0:T(8,128)}) custom-call(f32[128,128]{1,0:T(8,128)} %select_select_fusion.1.lower_a_ref, f32[128,128]{1,0:T(8,128)} %get-tuple-element.25.lower_b_ref, f32[128,128]{1,0:T(8,128)} %select_select_fusion.lower_c_ref, f32[128,128]{1,0:T(8,128)} %get-tuple-element.27.inv_a_ref, ...), custom_call_target="tpu_custom_call" | custom-call | tf_op jit(solution)/shard_map/pallas_call | solution.py:286
  299.6 9.0 %shard_map.74 = f32[768,2048]{1,0:T(8,128)} custom-call(f32[256,256]{1,0:T(8,128)} %get-tuple-element.29.inv_ref, f32[768,2048]{1,0:T(8,128)} %get-tuple-element.30.basis_ref), custom_call_target="tpu_custom_call" | custom-call | tf_op jit(solution)/shard_map/pallas_call | solution.py:139
  (38 shorter events, 1.8 us)
Async XLA Ops:
  4.8 25.6 %all-to-all-start.1 = ((s32[128,1,12]{2,1,0:T(1,128)}), s32[128,1,12]{2,1,0:T(1,128)S(1)}, u32[]{:S(2)}, u32[]{:S(2)}) async-start(s32[128,1,12]{2,1,0:T(1,128)} %bitcast.11), calls=%async_computation.1 | async-start | bytes 131072 | tf_op jit(solution)/shard_map/all_to_all | solution.py:322
  30.4 10.9 %copy-start.3 = (f32[2,9]{1,0:T(2,128)S(1)}, f32[2,9]{1,0:T(2,128)}, u32[]{:S(2)}) copy-start(f32[2,9]{1,0:T(2,128)} %taps_ref.1) | copy-start | bytes 220
  30.4 84.9 %all-to-all-start = ((bf16[128,12,16,128]{3,2,1,0:T(8,128)(2,1)}), bf16[128,12,16,128]{3,2,1,0:T(8,128)(2,1)}, u32[]{:S(2)}, u32[]{:S(2)}) async-start(bf16[128,12,16,128]{3,2,1,0:T(8,128)(2,1)} %bitcast.47), calls=%async_computation | async-start | bytes 12582912 | tf_op jit(solution)/shard_map/all_to_all | solution.py:315
  174.5 13.8 %copy-start = (f32[256,256]{1,0:T(8,128)}, f32[256,256]{1,0:T(8,128)S(1)}, u32[]{:S(2)}) copy-start(f32[256,256]{1,0:T(8,128)S(1)} %fusion.15.gram_ref) | copy-start | bytes 786436
  212.8 36.3 %copy-start.2 = (f32[256,256]{1,0:T(8,128)S(1)}, f32[256,256]{1,0:T(8,128)}, u32[]{:S(2)}) copy-start(f32[256,256]{1,0:T(8,128)} %get-tuple-element.28.first_ref) | copy-start | bytes 786436
  244.7 15.5 %all-to-all-start.5 = ((f32[128,1,512]{2,1,0:T(1,128)}), f32[128,1,512]{2,1,0:T(1,128)S(1)}, u32[]{:S(2)}, u32[]{:S(2)}) async-start(f32[128,1,512]{2,1,0:T(1,128)} %broadcast_in_dim.21), calls=%async_computation.5 | async-start | bytes 524288 | tf_op jit(solution)/shard_map/all_to_all | solution.py:296
  261.0 13.7 %copy-start.1 = (f32[256,256]{1,0:T(8,128)}, f32[256,256]{1,0:T(8,128)S(1)}, u32[]{:S(2)}) copy-start(f32[256,256]{1,0:T(8,128)S(1)} %fusion.14.gram_ref) | copy-start | bytes 786436

commit v8 on v7

--- a/solution.py
+++ b/solution.py
@@ -227,7 +227,8 @@
     inv_a_ref[...] = inv_a
     lower_b = nt_dot(gram_ref[half:, :half], inv_a)
     lower_b_ref[...] = lower_b
-    rest_ref[...] = gram_ref[half:, half:] - nt_dot(lower_b, lower_b)
+    far = gram_ref[half:, half:]
+    rest_ref[...] = (far + far.T) / 2 - nt_dot(lower_b, lower_b)
 
 
 def second_half_kernel(lower_a_ref, lower_b_ref, lower_c_ref, inv_a_ref, lower_ref, inverse_ref):
@@ -271,8 +272,8 @@
 def factor_and_inverse(gram, first=None, scale=1.0):
     size = gram.shape[0]
     half = size // 2
-    gram = (gram + gram.T) / 2
-    lower_a = lax.linalg.cholesky(gram[:half, :half], symmetrize_input=False)
+    corner = gram[:half, :half]
+    lower_a = lax.linalg.cholesky((corner + corner.T) / 2, symmetrize_input=False)
     square = jax.ShapeDtypeStruct((half, half), jnp.float32)
     inv_a, lower_b, rest = pl.pallas_call(
         first_half_kernel, out_shape=[square, square, square]

time: 314 us -> 314 us (level)
  no operation moved by 1% of the time
where the time goes in v8:
time: 314 us; the launch traced here: 309 us
  waiting for transfers between devices  81.4 us (26%)
  Pallas kernels  71.8 us (23%)
  other arithmetic  62.7 us (20%)
  blocking collectives  47.9 us (15%)
  starting transfers between devices  26.4 us (8%)
  matrix products  10.1 us (3%)
  local copies, waits for them, and re-layouts  7.24 us (2%)
    all_to_all x1, waiting for transfers between devices, local(): lax.all_to_all(buffer.reshape(devices_all, capacity, PX, PZ), ('gx', 'gy'...  71.2 us
    all_to_all x2, blocking collectives, sum_over_devices(): rows = lax.all_to_all(rows, axes, 0, 0, tiled=True)  32.2 us
    another operation x6, other arithmetic, factor_and_inverse(): lower_c = lax.linalg.cholesky(rest, symmetrize_input=False)  26.4 us
    another operation x6, other arithmetic, factor_and_inverse(): lax.linalg.cholesky((corner + corner.T) / 2, symmetrize_input=False)  24.9 us
    all_to_all x1, blocking collectives, sum_over_devices(): total = lax.all_to_all(total, axes, 0, 0, tiled=True)  15.7 us
    pallas_call x1, Pallas kernels, filter_planes(): pl.pallas_call(filter_kernel, grid=(count // SNAP,), in_specs=[pl.BlockSp...  14.6 us
    pallas_call x1, Pallas kernels, basis_and_gram(): pl.pallas_call(basis_kernel, grid=(count // size,), in_specs=[pl.BlockSpe...  14.3 us
    pallas_call x1, Pallas kernels, route_records(): pl.pallas_call(route_kernel, grid=(slots // rows,), in_specs=[pl.BlockSpe...  13.5 us
  transfers between devices with their start and end apart: 3, of which 2 were waited for; matrix products, arithmetic and copies ran while one was open for 1% of the time, Pallas kernels for 4%

profile of v8, /device:TPU:1, one launch (start us, length us, event | category | flops | bytes accessed | tf_op | source)
XLA Modules:
  0.0 308.7 jit_solution(10612484962767864955)
XLA Ops:
  0.6 0.8 copy.32
  1.8 1.0 fusion.13
  2.8 0.7 multiply_add_fusion
  3.5 0.6 select_reduce_fusion
  4.1 0.7 sub.36
  4.8 11.5 %all-to-all-start.1 = ((s32[128,1,12]{2,1,0:T(1,128)}), s32[128,1,12]{2,1,0:T(1,128)S(1)}, u32[]{:S(2)}, u32[]{:S(2)}) async-start(s32[128,1,12]{2,1,0:T(1,128)} %bitcast.11), calls=%async_computation.1 | async-start | bytes 131072 | tf_op jit(solution)/shard_map/all_to_all | solution.py:323
  16.3 0.6 reshape.173.slot_ref
  16.9 13.5 %shard_map.67 = bf16[1536,16,128]{2,1,0:T(8,128)(2,1)} custom-call(s32[1,768]{1,0:T(1,128)} %reshape.173.slot_ref, bf16[768,2048]{1,0:T(8,128)(2,1)} %records_ref.1), custom_call_target="tpu_custom_call" | custom-call | tf_op jit(solution)/shard_map/pallas_call | solution.py:165
  30.4 10.6 %all-to-all-start = ((bf16[128,12,16,128]{3,2,1,0:T(8,128)(2,1)}), bf16[128,12,16,128]{3,2,1,0:T(8,128)(2,1)}, u32[]{:S(2)}, u32[]{:S(2)}) async-start(bf16[128,12,16,128]{3,2,1,0:T(8,128)(2,1)} %bitcast.47), calls=%async_computation | async-start | bytes 12582912 | tf_op jit(solution)/shard_map/all_to_all | solution.py:316
  41.1 0.2 iota_compare_fusion.2
  41.3 0.5 fusion.9
  42.0 0.7 pad_maximum_fusion.span_ref
  42.7 0.5 compare_reduce_fusion
  43.4 0.5 divide_reduce_fusion
  44.2 71.2 %all-to-all-done = bf16[128,12,16,128]{3,2,1,0:T(8,128)(2,1)} async-done(((bf16[128,12,16,128]{3,2,1,0:T(8,128)(2,1)}), bf16[128,12,16,128]{3,2,1,0:T(8,128)(2,1)}, u32[]{:S(2)}, u32[]{:S(2)}) %all-to-all-start) | async-done | bytes 6291488 | tf_op jit(solution)/shard_map/all_to_all | solution.py:316
  115.4 9.5 %convert_bitcast_fusion.planes_ref = bf16[16,768,128]{2,1,0:T(8,128)(2,1)} fusion(s32[1536]{0:T(1024)S(1)} %fusion.25, bf16[1536,16,128]{2,1,0:T(8,128)(2,1)} %bitcast.10), kind=kOutput, calls=%fused_computation.6 | convolution fusion | flops 4834590720 | bytes 9443328 | tf_op jit(solution)/shard_map/tk,kab->atb/dot_general | solution.py:336
  124.9 14.6 %shard_map.68 = (f32[768,2048]{1,0:T(8,128)}, f32[256,256]{1,0:T(8,128)}) custom-call(f32[2,9]{1,0:T(2,128)} %taps_ref.1, bf16[128,384]{1,0:T(8,128)(2,1)} %pad_maximum_fusion.span_ref, bf16[16,768,128]{2,1,0:T(8,128)(2,1)} %convert_bitcast_fusion.planes_ref), custom_call_target="tpu_custom_call" | custom-call | tf_op jit(solution)/shard_map/pallas_call | solution.py:62
  139.4 1.2 all_to_all.35
  140.7 16.9 %all_to_all.43 = f32[128,1,512]{2,1,0:T(1,128)S(1)} all-to-all(f32[128,1,512]{2,1,0:T(1,128)S(1)} %all_to_all.35), channel_id=1, replica_groups=mesh['gx'=8,'gy'=16] {'gx','gy'}, dimensions={0} | all-to-all | bytes 524288 | tf_op jit(solution)/shard_map/all_to_all | solution.py:294
  157.6 0.2 reduce_sum.38
  158.0 15.7 %all_to_all.44 = f32[128,1,512]{2,1,0:T(1,128)S(1)} all-to-all(f32[128,1,512]{2,1,0:T(1,128)S(1)} %broadcast_in_dim.20), channel_id=1, replica_groups=mesh['gx'=8,'gy'=16] {'gx','gy'}, dimensions={0} | all-to-all | bytes 524288 | tf_op jit(solution)/shard_map/all_to_all | solution.py:297
  173.7 0.6 reduce.42
  174.5 11.7 %custom-call.6 = f32[128,128]{1,0:T(8,128)S(1)} custom-call(f32[128,128]{1,0:T(8,128)S(1)} %fusion.17), custom_call_target="Cholesky" | custom-call | tf_op jit(solution)/shard_map/cholesky/custom-call.1 | solution.py:276
  186.2 0.7 compare_reduce_fusion.5
  187.0 1.3 select_select_fusion.3.lower_a_ref
  188.3 5.2 %shard_map.69 = (f32[128,128]{1,0:T(8,128)}, f32[128,128]{1,0:T(8,128)}, f32[128,128]{1,0:T(8,128)}) custom-call(f32[128,128]{1,0:T(8,128)} %select_select_fusion.3.lower_a_ref, f32[256,256]{1,0:T(8,128)} %copy-done), custom_call_target="tpu_custom_call" | custom-call | tf_op jit(solution)/shard_map/pallas_call | solution.py:278
  193.5 12.5 %custom-call.7 = f32[128,128]{1,0:T(8,128)S(1)} custom-call(f32[128,128]{1,0:T(8,128)} %get-tuple-element.20), custom_call_target="Cholesky" | custom-call | tf_op jit(solution)/shard_map/cholesky/custom-call.1 | solution.py:281
  206.1 0.6 compare_reduce_fusion.4
  206.7 1.3 select_select_fusion.2.lower_c_ref
  208.0 4.8 %shard_map.70 = (f32[256,256]{1,0:T(8,128)}, f32[256,256]{1,0:T(8,128)}) custom-call(f32[128,128]{1,0:T(8,128)} %select_select_fusion.3.lower_a_ref, f32[128,128]{1,0:T(8,128)} %get-tuple-element.19.lower_b_ref, f32[128,128]{1,0:T(8,128)} %select_select_fusion.2.lower_c_ref, f32[128,128]{1,0:T(8,128)} %get-tuple-element.21.inv_a_ref), custom_call_target="tpu_custom_call" | custom-call | tf_op jit(solution)/shard_map/pallas_call | solution.py:284
  212.7 14.3 %shard_map.71 = (f32[768,2048]{1,0:T(8,128)}, f32[256,256]{1,0:T(8,128)}) custom-call(f32[256,256]{1,0:T(8,128)} %get-tuple-element.22.inv_ref, f32[768,2048]{1,0:T(8,128)} %get-tuple-element.23.matrix_ref), custom_call_target="tpu_custom_call" | custom-call | tf_op jit(solution)/shard_map/pallas_call | solution.py:106
  227.1 1.2 all_to_all.36
  228.3 15.3 %all_to_all.45 = f32[128,1,512]{2,1,0:T(1,128)S(1)} all-to-all(f32[128,1,512]{2,1,0:T(1,128)S(1)} %all_to_all.36), channel_id=1, replica_groups=mesh['gx'=8,'gy'=16] {'gx','gy'}, dimensions={0} | all-to-all | bytes 524288 | tf_op jit(solution)/shard_map/all_to_all | solution.py:294
  243.6 0.2 reduce_sum.39
  243.8 0.8 broadcast_in_dim.21
  244.6 4.4 %all-to-all-start.5 = ((f32[128,1,512]{2,1,0:T(1,128)}), f32[128,1,512]{2,1,0:T(1,128)S(1)}, u32[]{:S(2)}, u32[]{:S(2)}) async-start(f32[128,1,512]{2,1,0:T(1,128)} %broadcast_in_dim.21), calls=%async_computation.5 | async-start | bytes 524288 | tf_op jit(solution)/shard_map/all_to_all | solution.py:297
  249.0 0.8 copy.42
  249.9 10.2 %all-to-all-done.5 = f32[128,1,512]{2,1,0:T(1,128)S(1)} async-done(((f32[128,1,512]{2,1,0:T(1,128)}), f32[128,1,512]{2,1,0:T(1,128)S(1)}, u32[]{:S(2)}, u32[]{:S(2)}) %all-to-all-start.5) | async-done | bytes 262176 | tf_op jit(solution)/shard_map/all_to_all | solution.py:297
  260.1 0.6 reduce.43
  260.9 11.7 %custom-call.8 = f32[128,128]{1,0:T(8,128)S(1)} custom-call(f32[128,128]{1,0:T(8,128)S(1)} %fusion.16), custom_call_target="Cholesky" | custom-call | tf_op jit(solution)/shard_map/cholesky/custom-call.1 | solution.py:276
  272.7 0.6 compare_reduce_fusion.3
  273.3 1.3 select_select_fusion.1.lower_a_ref
  274.6 5.2 %shard_map.72 = (f32[128,128]{1,0:T(8,128)}, f32[128,128]{1,0:T(8,128)}, f32[128,128]{1,0:T(8,128)}) custom-call(f32[128,128]{1,0:T(8,128)} %select_select_fusion.1.lower_a_ref, f32[256,256]{1,0:T(8,128)} %copy-done.1), custom_call_target="tpu_custom_call" | custom-call | tf_op jit(solution)/shard_map/pallas_call | solution.py:278
  279.8 12.5 %custom-call.9 = f32[128,128]{1,0:T(8,128)S(1)} custom-call(f32[128,128]{1,0:T(8,128)} %get-tuple-element.26), custom_call_target="Cholesky" | custom-call | tf_op jit(solution)/shard_map/cholesky/custom-call.1 | solution.py:281
  292.4 0.6 compare_reduce_fusion.2
  293.0 1.3 select_select_fusion.lower_c_ref
  294.3 5.2 %shard_map.73 = (f32[256,256]{1,0:T(8,128)}, f32[256,256]{1,0:T(8,128)}, f32[256,256]{1,0:T(8,128)}) custom-call(f32[128,128]{1,0:T(8,128)} %select_select_fusion.1.lower_a_ref, f32[128,128]{1,0:T(8,128)} %get-tuple-element.25.lower_b_ref, f32[128,128]{1,0:T(8,128)} %select_select_fusion.lower_c_ref, f32[128,128]{1,0:T(8,128)} %get-tuple-element.27.inv_a_ref, ...), custom_call_target="tpu_custom_call" | custom-call | tf_op jit(solution)/shard_map/pallas_call | solution.py:287
  299.5 9.0 %shard_map.74 = f32[768,2048]{1,0:T(8,128)} custom-call(f32[256,256]{1,0:T(8,128)} %get-tuple-element.29.inv_ref, f32[768,2048]{1,0:T(8,128)} %get-tuple-element.30.basis_ref), custom_call_target="tpu_custom_call" | custom-call | tf_op jit(solution)/shard_map/pallas_call | solution.py:139
  (38 shorter events, 1.6 us)
Async XLA Ops:
  4.8 25.6 %all-to-all-start.1 = ((s32[128,1,12]{2,1,0:T(1,128)}), s32[128,1,12]{2,1,0:T(1,128)S(1)}, u32[]{:S(2)}, u32[]{:S(2)}) async-start(s32[128,1,12]{2,1,0:T(1,128)} %bitcast.11), calls=%async_computation.1 | async-start | bytes 131072 | tf_op jit(solution)/shard_map/all_to_all | solution.py:323
  30.4 10.9 %copy-start.3 = (f32[2,9]{1,0:T(2,128)S(1)}, f32[2,9]{1,0:T(2,128)}, u32[]{:S(2)}) copy-start(f32[2,9]{1,0:T(2,128)} %taps_ref.1) | copy-start | bytes 220
  30.4 84.9 %all-to-all-start = ((bf16[128,12,16,128]{3,2,1,0:T(8,128)(2,1)}), bf16[128,12,16,128]{3,2,1,0:T(8,128)(2,1)}, u32[]{:S(2)}, u32[]{:S(2)}) async-start(bf16[128,12,16,128]{3,2,1,0:T(8,128)(2,1)} %bitcast.47), calls=%async_computation | async-start | bytes 12582912 | tf_op jit(solution)/shard_map/all_to_all | solution.py:316
  174.4 13.9 %copy-start = (f32[256,256]{1,0:T(8,128)}, f32[256,256]{1,0:T(8,128)S(1)}, u32[]{:S(2)}) copy-start(f32[256,256]{1,0:T(8,128)S(1)} %reshape.176.gram_ref) | copy-start | bytes 786436
  212.7 36.3 %copy-start.2 = (f32[256,256]{1,0:T(8,128)S(1)}, f32[256,256]{1,0:T(8,128)}, u32[]{:S(2)}) copy-start(f32[256,256]{1,0:T(8,128)} %get-tuple-element.28.first_ref) | copy-start | bytes 786436
  244.6 15.5 %all-to-all-start.5 = ((f32[128,1,512]{2,1,0:T(1,128)}), f32[128,1,512]{2,1,0:T(1,128)S(1)}, u32[]{:S(2)}, u32[]{:S(2)}) async-start(f32[128,1,512]{2,1,0:T(1,128)} %broadcast_in_dim.21), calls=%async_computation.5 | async-start | bytes 524288 | tf_op jit(solution)/shard_map/all_to_all | solution.py:297
  260.8 13.8 %copy-start.1 = (f32[256,256]{1,0:T(8,128)}, f32[256,256]{1,0:T(8,128)S(1)}, u32[]{:S(2)}) copy-start(f32[256,256]{1,0:T(8,128)S(1)} %reshape.177.gram_ref) | copy-start | bytes 786436
